TPU v7x, 256 devices: a whole 4x4x8 slice. The times are simulated.
256 devices in a mesh: ctx: 8 (over z_lo, core), exp: 32 (over y, x, z_hi).
Axes of the slice: x: 4, y: 4, z: 8 (z_hi: 2, z_lo: 4; z = z_hi * 4 + z_lo), core: 2. Of those that a mesh axis runs over, the one named last changes fastest.
Arguments:
- queries: bfloat16 [32, 64, 6144], P('exp', None, 'ctx'), may hold values from -18 to 18
- cached_keys: bfloat16 [32, 1024, 1024], P('exp', 'ctx'), may hold values from -6 to 6
- cached_values: bfloat16 [32, 1024, 1024], P('exp', 'ctx'), may hold values from -6 to 6
- fresh_keys: bfloat16 [32, 64, 1024], P('exp', None, 'ctx'), may hold values from -6 to 6
- fresh_values: bfloat16 [32, 64, 1024], P('exp', None, 'ctx'), may hold values from -6 to 6
- slot_order: int32 [32, 64], P('exp'), may hold values from 0 to 63, each once within a row
- residual: bfloat16 [32, 64, 6144], P('exp'), may hold values from -6 to 6
- expert_ids: int32 [32, 64, 2], P('exp'), may hold values from 0 to 3, all different within a row; in each aligned block of 64 rows (0 to 63, 64 to 127, ..., all dimensions but the last counted through in order) at most 32 rows name the same one
- gate_num: int32 [32, 64, 2], P('exp'), may hold values from 32 to 224, as said below
- gain_attn: float32 [6144], replicated, may hold values from 0.1 to 1.9
- gain_pre: float32 [6144], replicated, may hold values from 0.1 to 1.9
- gain_post: float32 [6144], replicated, may hold values from 0.1 to 1.9
- w_gate: bfloat16 [32, 6144, 2048], P('exp', None, 'ctx'), may hold values from -0.078125 to 0.078125
- w_up: bfloat16 [32, 6144, 2048], P('exp', None, 'ctx'), may hold values from -0.078125 to 0.078125
- w_down: bfloat16 [32, 2048, 6144], P('exp', 'ctx'), may hold values from -0.046875 to 0.046875
Outputs:
- layer_out: bfloat16 [32, 64, 6144], P('exp')
Inputs may be any that keep to these rules, and one draw needn't show every extreme that they name: `expert_ids`: each token names 2 different experts; the tokens of one request name each expert exactly 32 times. `gate_num`: the two numbers of a token sum to 256. `slot_order`: within one request the slots of the new tokens are a permutation.
All inputs are finite; a program needn't handle non-finite values.
Results may differ from a plain program's by a relative error of at most 0.012.
Values may be sent and summed in bfloat16 or wider, within the bound.
No kernel may reach another device: no remote copies, remote signals or barrier semaphores. Data moves between devices by JAX's collectives and lax.ppermute only.
A program may use at most 128 MiB of HBM per device.

v0:
```python
import jax
import jax.numpy as jnp
from jax import lax
from jax.sharding import PartitionSpec as P

D = 6144
HEAD_SIZE = 128
EXPERTS = 4
CAP = 32


def normalize(values, scaling):
    return values * lax.rsqrt(jnp.mean(values * values, axis=-1, keepdims=True) + 1e-05) * scaling


def route_tables(expert_ids, gate_num):
    blocks = expert_ids.shape[0]
    per_block = expert_ids.shape[1]
    top_k = expert_ids.shape[2]
    flat_ids = expert_ids.reshape(blocks, per_block * top_k)
    onehot = (flat_ids[..., None] == jnp.arange(EXPERTS, dtype=jnp.int32)).astype(jnp.int32)
    before = jnp.cumsum(onehot, axis=1) - onehot
    slot_num = jnp.sum(onehot * before, axis=-1)
    target = flat_ids * CAP + slot_num
    one_table = (target[..., None] == jnp.arange(EXPERTS * CAP, dtype=jnp.int32)).astype(
        jnp.float32
    )
    one_table = one_table.reshape(blocks, per_block, top_k, EXPERTS * CAP)
    fractions = gate_num.astype(jnp.float32) / 256.0
    dispatch = jnp.sum(one_table, axis=2)
    combine = jnp.sum(one_table * fractions[..., None], axis=2)
    return (dispatch, combine)


def attend_part(query_row_block, query_slot, key_row_block, value_row_block, key_slot):
    query_count = query_row_block.shape[0]
    key_count = key_row_block.shape[0]
    n_kv = key_row_block.shape[1] // HEAD_SIZE
    query_groups = query_row_block.shape[1] // HEAD_SIZE // n_kv
    query_head_rows = query_row_block.reshape(query_count, n_kv, query_groups, HEAD_SIZE)
    key_head_rows = key_row_block.reshape(key_count, n_kv, HEAD_SIZE)
    value_head_rows = value_row_block.reshape(key_count, n_kv, HEAD_SIZE)
    scores = jnp.einsum(
        "qhgd,khd->hgqk", query_head_rows, key_head_rows, preferred_element_type=jnp.float32
    ) * HEAD_SIZE ** (-0.5)
    capped = 30.0 * jnp.tanh(scores / 30.0)
    visible = key_slot[None, None, None, :] <= query_slot[None, None, :, None]
    attn_weights = jnp.where(visible, jnp.exp(capped), 0.0).astype(jnp.bfloat16)
    totals = jnp.sum(attn_weights.astype(jnp.float32), axis=-1)
    totals = jnp.transpose(totals, (2, 0, 1)).reshape(query_count, n_kv * query_groups)
    numerator = jnp.einsum(
        "hgqk,khd->qhgd", attn_weights, value_head_rows, preferred_element_type=jnp.float32
    )
    return (numerator.reshape(query_count, n_kv * query_groups * HEAD_SIZE), totals)


def per_device(
    queries,
    cached_keys,
    cached_values,
    fresh_keys,
    fresh_values,
    slot_order,
    residual,
    expert_ids,
    gate_num,
    gain_attn,
    gain_pre,
    gain_post,
    w_gate,
    w_up,
    w_down,
):
    query_row_block = queries[0]
    query_count = query_row_block.shape[0]
    query_slot = slot_order[0].astype(jnp.float32)
    head_width = fresh_keys.shape[2]
    new_numer, new_totals = attend_part(
        query_row_block, query_slot, fresh_keys[0], fresh_values[0], query_slot
    )
    column_start = lax.axis_index("ctx") * head_width
    key_part = lax.dynamic_slice_in_dim(
        lax.all_gather(cached_keys[0], "ctx", axis=0, tiled=True), column_start, head_width, 1
    )
    value_part = lax.dynamic_slice_in_dim(
        lax.all_gather(cached_values[0], "ctx", axis=0, tiled=True), column_start, head_width, 1
    )
    cache_slot = jnp.full((key_part.shape[0],), -1.0, jnp.float32)
    numer_part, total_part = attend_part(
        query_row_block, query_slot, key_part, value_part, cache_slot
    )
    numerator = new_numer + numer_part
    totals = new_totals + total_part
    local_heads = (numerator.reshape(query_count, -1, HEAD_SIZE) / totals[..., None]).reshape(
        query_count, -1
    )
    attended = lax.all_gather(local_heads, "ctx", axis=1, tiled=True)
    hidden_state = (residual[0].astype(jnp.float32) + normalize(attended, gain_attn)).astype(
        jnp.bfloat16
    )
    normed = normalize(hidden_state.astype(jnp.float32), gain_pre).astype(jnp.bfloat16)
    dispatch, combine = route_tables(expert_ids, gate_num)
    buffer = jnp.einsum(
        "ns,nd->sd", dispatch[0].astype(jnp.bfloat16), normed, preferred_element_type=jnp.float32
    ).astype(jnp.bfloat16)
    split_count = lax.axis_size("exp") // EXPERTS
    gate_mat = w_gate[0]
    up_mat = w_up[0]
    down_mat = w_down[0]
    spread = jnp.broadcast_to(
        buffer.reshape(EXPERTS, 1, CAP, D), (EXPERTS, split_count, CAP, D)
    ).reshape(EXPERTS * split_count, CAP, D)
    row_block = lax.all_to_all(spread, "exp", split_axis=0, concat_axis=0, tiled=True)
    flat_rows = row_block.reshape(-1, D)
    pre_gate = jnp.dot(flat_rows, gate_mat, preferred_element_type=jnp.float32)
    pre_up = jnp.dot(flat_rows, up_mat, preferred_element_type=jnp.float32)
    hidden_units = (jax.nn.gelu(pre_gate) * pre_up).astype(jnp.bfloat16)
    projected = jnp.dot(hidden_units, down_mat, preferred_element_type=jnp.float32).astype(
        jnp.bfloat16
    )
    computed = projected.reshape(row_block.shape)
    returned = lax.all_to_all(computed, "exp", split_axis=0, concat_axis=0, tiled=True)
    split_total = jnp.sum(
        returned.astype(jnp.float32).reshape(EXPERTS, split_count, CAP, D), axis=1
    ).reshape(EXPERTS * CAP, D)
    expert_out = lax.psum(split_total, "ctx")
    mixture = jnp.dot(combine[0], expert_out, precision=lax.Precision.HIGHEST)
    layer_out = hidden_state.astype(jnp.float32) + normalize(mixture, gain_post)
    return layer_out.astype(jnp.bfloat16)[None]


def solution(mesh):
    in_specs = (
        P("exp", None, "ctx"),
        P("exp", "ctx", None),
        P("exp", "ctx", None),
        P("exp", None, "ctx"),
        P("exp", None, "ctx"),
        P("exp", None),
        P("exp", None, None),
        P("exp", None, None),
        P("exp", None, None),
        P(),
        P(),
        P(),
        P("exp", None, "ctx"),
        P("exp", None, "ctx"),
        P("exp", "ctx", None),
    )
    out_specs = P("exp", None, None)
    return jax.shard_map(
        per_device, mesh=mesh, in_specs=in_specs, out_specs=out_specs, check_vma=False
    )
```

profile of v0, /device:TPU:1, one launch (start us, length us, event | category | flops | bytes accessed | tf_op | source)
XLA Modules:
  0.0 817.5 jit_solution(1975805904327731259)
XLA Ops:
  6.5 0.7 all-gather.10.cloned.1.call-update
  8.1 1.0 reshape.340
  10.5 1.0 convert_reduce_fusion.2
  11.5 0.9 convolution_bitcast_fusion
  12.4 37.7 %all-gather.10.cloned.1.call-done = bf16[1,1024,1024]{2,1,0:T(8,128)(2,1)} async-done(((bf16[1,128,1024]{2,1,0:T(8,128)(2,1)}), bf16[1,1024,1024]{2,1,0:T(8,128)(2,1)}) %all-gather.10.cloned.1.call-update) | async-done | bytes 2097168 | tf_op jit(solution)/shard_map/all_gather | solution.py:83
  50.1 2.4 convert_reduce_fusion.1
  52.6 37.5 %all-gather.8.cloned.1.call-done = bf16[1,1024,1024]{2,1,0:T(8,128)(2,1)} async-done(((bf16[1,128,1024]{2,1,0:T(8,128)(2,1)}), bf16[1,1024,1024]{2,1,0:T(8,128)(2,1)}) %all-gather.8.cloned.1.call-update) | async-done | bytes 2097168 | tf_op jit(solution)/shard_map/all_gather | solution.py:86
  90.2 1.6 fusion.19
  92.1 0.8 bitcast_divide_fusion
  93.9 35.8 %all-gather.6.cloned.1.call-done = f32[64,6144]{1,0:T(8,128)} async-done(((f32[64,768]{1,0:T(8,128)}), f32[64,6144]{1,0:T(8,128)}) %all-gather.6.cloned.1.call-update) | async-done | bytes 1572880 | tf_op jit(solution)/shard_map/all_gather | solution.py:97
  129.8 1.7 multiply_reduce_fusion.1
  131.6 1.6 fusion.5
  133.3 0.9 copy-done.3
  134.2 1.8 convolution_convert_fusion.1
  136.0 7.5 broadcast_in_dim.53
  143.6 288.1 %all_to_all.10 = bf16[32,32,6144]{2,1,0:T(8,128)(2,1)S(1)} all-to-all(bf16[32,32,6144]{2,1,0:T(8,128)(2,1)} %bitcast.108), channel_id=1, replica_groups=mesh['ctx'=8,'exp'=32] {'exp'}, dimensions={0} | all-to-all | bytes 25165824 | tf_op jit(solution)/shard_map/all_to_all | solution.py:113
  431.6 4.5 copy-done.2
  436.1 4.6 fusion.32
  440.7 19.8 %convolution_convert_fusion = bf16[1024,6144]{1,0:T(8,128)(2,1)} fusion(bf16[1,256,6144]{2,1,0:T(8,128)(2,1)S(1)} %copy-done, f32[1024,256]{1,0:T(8,128)} %fusion.32, bf16[1024,6144]{1,0:T(8,128)(2,1)} %bitcast.106, bf16[1,6144,256]{2,1,0:T(8,128)(2,1)} %param.28), kind=kOutput, calls=%fused_computation.1 | convolution fusion | flops 6449266688 | bytes 32505856 | tf_op jit(solution)/shard_map/dot_general | solution.py:118
  460.6 246.8 %all_to_all.11 = bf16[32,32,6144]{2,1,0:T(8,128)(2,1)} all-to-all(bf16[32,32,6144]{2,1,0:T(8,128)(2,1)} %bitcast.107), channel_id=1, replica_groups=mesh['ctx'=8,'exp'=32] {'exp'}, dimensions={0} | all-to-all | bytes 25165824 | tf_op jit(solution)/shard_map/all_to_all | solution.py:122
  707.4 8.7 %convert_reduce_fusion = f32[4,32,6144]{2,1,0:T(8,128)} fusion(bf16[32,32,6144]{2,1,0:T(8,128)(2,1)} %all_to_all.11), kind=kLoop, calls=%fused_computation | loop fusion | flops 11796480 | bytes 15728640 | tf_op jit(solution)/shard_map/reduce_sum | solution.py:123
  716.1 89.6 %all-reduce.2.cloned.1.call-done = f32[128,6144]{1,0:T(8,128)} async-done(((f32[128,6144]{1,0:T(8,128)}), f32[128,6144]{1,0:T(8,128)}) %all-reduce.2.cloned.1.call-update) | async-done | bytes 3145744 | tf_op jit(solution)/shard_map/psum | solution.py:126
  805.7 4.0 multiply_reduce_fusion
  809.7 1.2 fusion.35
  (49 shorter events, 3.8 us)
Async XLA Ops:
  6.5 434.2 %copy-start = (bf16[1,256,6144]{2,1,0:T(8,128)(2,1)S(1)}, bf16[1,256,6144]{2,1,0:T(8,128)(2,1)}, u32[]{:S(2)}) copy-start(bf16[1,256,6144]{2,1,0:T(8,128)(2,1)} %param.29) | copy-start | bytes 9437188
  6.5 43.5 %all-gather.10.cloned.1.call-start = ((), (), s32[]{:S(2)}) async-start(), calls=%async_computation.5 | async-start | bytes 2359296 | tf_op jit(solution)/shard_map/all_gather | solution.py:83
  7.3 82.9 %all-gather.8.cloned.1.call-start = ((), (), s32[]{:S(2)}) async-start(), calls=%async_computation.4 | async-start | bytes 2359296 | tf_op jit(solution)/shard_map/all_gather | solution.py:86
  8.0 121.8 %all-gather.6.cloned.1.call-start = ((), (), s32[]{:S(2)}) async-start(), calls=%async_computation.2 | async-start | bytes 1769472 | tf_op jit(solution)/shard_map/all_gather | solution.py:97
  52.5 40.4 %copy-start.9 = (s32[1,64,2]{1,2,0:T(2,128)S(1)}, s32[1,64,2]{1,2,0:T(2,128)}, u32[]{:S(2)}) copy-start(s32[1,64,2]{1,2,0:T(2,128)} %param.22) | copy-start | bytes 1540
  52.5 41.3 %copy-start.10 = (s32[1,64,2]{1,2,0:T(2,128)S(1)}, s32[1,64,2]{1,2,0:T(2,128)}, u32[]{:S(2)}) copy-start(s32[1,64,2]{1,2,0:T(2,128)} %param.23) | copy-start | bytes 1540
  91.8 39.7 %copy-start.6 = (f32[6144]{0:T(1024)S(1)}, f32[6144]{0:T(1024)}, u32[]{:S(2)}) copy-start(f32[6144]{0:T(1024)} %param.24) | copy-start | bytes 73732
  92.8 712.9 %all-reduce.2.cloned.1.call-start = ((), (), s32[]{:S(2)}) async-start(), calls=%async_computation.3 | async-start | bytes 6291456 | tf_op jit(solution)/shard_map/psum | solution.py:126
  129.8 1.9 copy-start.5
  129.8 4.4 copy-start.7
  133.3 0.9 copy-start.3
  143.6 292.5 %copy-start.11 = (bf16[1,6144,256]{2,1,0:T(8,128)(2,1)S(1)}, bf16[1,6144,256]{2,1,0:T(8,128)(2,1)}, u32[]{:S(2)}) copy-start(bf16[1,6144,256]{2,1,0:T(8,128)(2,1)} %param.27) | copy-start | bytes 9437188
  431.6 4.5 copy-start.2
  805.7 4.0 copy-start.4
  805.7 4.0 copy-start.8
  805.7 5.2 copy-start.1
Sparse Core Ops, SparseCore 0:
  9.1 40.9 all-gather.9
  51.9 38.2 all-gather.7
  93.0 36.7 all-gather.5
  716.2 89.4 all-reduce.1
where the time goes:
time: 818 us; the launch traced here: 817 us
  blocking collectives  535 us (65%)
  waiting for transfers between devices  202 us (25%)
  matrix products  36.2 us (4%)
  other arithmetic  16 us (2%)
  local copies, waits for them, and re-layouts  14.9 us (2%)
  between operations  13.3 us (2%)
    all_to_all x1, blocking collectives, per_device(): lax.all_to_all(spread, 'exp', split_axis=0, concat_axis=0, tiled=True)  288 us
    all_to_all x1, blocking collectives, per_device(): lax.all_to_all(computed, 'exp', split_axis=0, concat_axis=0, tiled=True)  247 us
    psum x1, waiting for transfers between devices, per_device(): expert_out = lax.psum(split_total, 'ctx')  89.6 us
    all_gather x1, waiting for transfers between devices, per_device(): lax.all_gather(cached_keys[0], 'ctx', axis=0, tiled=True)  37.7 us
    all_gather x1, waiting for transfers between devices, per_device(): lax.all_gather(cached_values[0], 'ctx', axis=0, tiled=True)  37.5 us
    all_gather x1, waiting for transfers between devices, per_device(): attended = lax.all_gather(local_heads, 'ctx', axis=1, tiled=True)  35.8 us
    dot_general x1, matrix products, per_device(): jnp.dot(hidden_units, down_mat, preferred_element_type=jnp.float32)  19.8 us
  transfers between devices with their start and end apart: 4, of which 4 were waited for; matrix products, arithmetic and copies ran while one was open for 1% of the time, Pallas kernels for 0%

commit v1 on v0

v1 whole, which is shorter than its diff:
```python
import jax
import jax.numpy as jnp
import numpy as np
from jax import lax
from jax.sharding import Mesh
from jax.sharding import PartitionSpec as P

D = 6144
HEAD_SIZE = 128
EXPERTS = 4
CAP = 32
EPS = 1e-05

CTX = ("zl", "core")
REQ = ("y", "x", "zh")


def route_tables(expert_ids, gate_num):
    blocks = expert_ids.shape[0]
    per_block = expert_ids.shape[1]
    top_k = expert_ids.shape[2]
    flat_ids = expert_ids.reshape(blocks, per_block * top_k)
    onehot = (flat_ids[..., None] == jnp.arange(EXPERTS, dtype=jnp.int32)).astype(jnp.int32)
    before = jnp.cumsum(onehot, axis=1) - onehot
    slot_num = jnp.sum(onehot * before, axis=-1)
    target = flat_ids * CAP + slot_num
    one_table = (target[..., None] == jnp.arange(EXPERTS * CAP, dtype=jnp.int32)).astype(
        jnp.float32
    )
    one_table = one_table.reshape(blocks, per_block, top_k, EXPERTS * CAP)
    fractions = gate_num.astype(jnp.float32) / 256.0
    dispatch = jnp.sum(one_table, axis=2)
    combine = jnp.sum(one_table * fractions[..., None], axis=2)
    return (dispatch, combine)


def attend_part(query_row_block, query_slot, key_row_block, value_row_block, key_slot):
    query_count = query_row_block.shape[0]
    key_count = key_row_block.shape[0]
    n_kv = key_row_block.shape[1] // HEAD_SIZE
    query_groups = query_row_block.shape[1] // HEAD_SIZE // n_kv
    query_head_rows = query_row_block.reshape(query_count, n_kv, query_groups, HEAD_SIZE)
    key_head_rows = key_row_block.reshape(key_count, n_kv, HEAD_SIZE)
    value_head_rows = value_row_block.reshape(key_count, n_kv, HEAD_SIZE)
    scores = jnp.einsum(
        "qhgd,khd->hgqk", query_head_rows, key_head_rows, preferred_element_type=jnp.float32
    ) * HEAD_SIZE ** (-0.5)
    capped = 30.0 * jnp.tanh(scores / 30.0)
    visible = key_slot[None, None, None, :] <= query_slot[None, None, :, None]
    attn_weights = jnp.where(visible, jnp.exp(capped), 0.0).astype(jnp.bfloat16)
    totals = jnp.sum(attn_weights.astype(jnp.float32), axis=-1)
    totals = jnp.transpose(totals, (2, 0, 1)).reshape(query_count, n_kv * query_groups)
    numerator = jnp.einsum(
        "hgqk,khd->qhgd", attn_weights, value_head_rows, preferred_element_type=jnp.float32
    )
    return (numerator.reshape(query_count, n_kv * query_groups * HEAD_SIZE), totals)


def col_slice(values, width):
    start = lax.axis_index(CTX) * width
    return lax.dynamic_slice_in_dim(values, start, width, values.ndim - 1)


def row_scale(local_rows, gain_cols):
    sum_sq = lax.psum(jnp.sum(local_rows * local_rows, axis=-1, keepdims=True), CTX)
    return local_rows * lax.rsqrt(sum_sq / D + EPS) * gain_cols


def per_device(
    queries,
    cached_keys,
    cached_values,
    fresh_keys,
    fresh_values,
    slot_order,
    residual,
    expert_ids,
    gate_num,
    gain_attn,
    gain_pre,
    gain_post,
    w_gate,
    w_up,
    w_down,
):
    query_row_block = queries[0]
    query_count = query_row_block.shape[0]
    width = query_row_block.shape[1]
    query_slot = slot_order[0].astype(jnp.float32)
    head_width = fresh_keys.shape[2]
    n_ctx = D // width

    with jax.named_scope("attention"):
        new_numer, new_totals = attend_part(
            query_row_block, query_slot, fresh_keys[0], fresh_values[0], query_slot
        )
        cache_rows = cached_keys.shape[1]
        key_heads = cached_keys[0].reshape(cache_rows, n_ctx, head_width)
        value_heads = cached_values[0].reshape(cache_rows, n_ctx, head_width)
        key_part = lax.all_to_all(key_heads, CTX, split_axis=1, concat_axis=0, tiled=True)
        value_part = lax.all_to_all(value_heads, CTX, split_axis=1, concat_axis=0, tiled=True)
        key_part = key_part.reshape(-1, head_width)
        value_part = value_part.reshape(-1, head_width)
        cache_slot = jnp.full((key_part.shape[0],), -1.0, jnp.float32)
        numer_part, total_part = attend_part(
            query_row_block, query_slot, key_part, value_part, cache_slot
        )
        numerator = new_numer + numer_part
        totals = new_totals + total_part
        local_heads = (
            numerator.reshape(query_count, -1, HEAD_SIZE) / totals[..., None]
        ).reshape(query_count, -1)

    with jax.named_scope("norms"):
        residual_cols = col_slice(residual[0], width).astype(jnp.float32)
        hidden_cols = (residual_cols + row_scale(local_heads, col_slice(gain_attn, width))).astype(
            jnp.bfloat16
        )
        normed_cols = row_scale(hidden_cols.astype(jnp.float32), col_slice(gain_pre, width)).astype(
            jnp.bfloat16
        )

    dispatch, combine = route_tables(expert_ids, gate_num)
    with jax.named_scope("dispatch"):
        buffer = jnp.einsum(
            "ns,nd->sd",
            dispatch[0].astype(jnp.bfloat16),
            normed_cols,
            preferred_element_type=jnp.float32,
        ).astype(jnp.bfloat16)
        rows = buffer.reshape(EXPERTS, CAP, width)
        rows = lax.all_to_all(rows, "y", split_axis=0, concat_axis=0, tiled=True)
        rows = lax.all_gather(rows, ("zh", "zl"), axis=0, tiled=False)
        rows = lax.all_gather(rows, "x", axis=0, tiled=False)
        rows = lax.all_gather(rows, "core", axis=0, tiled=False)
        n_core, n_x, n_z, n_y = rows.shape[:4]
        n_zh = 2
        n_zl = n_z // n_zh
        rows = rows.reshape(n_core, n_x, n_zh, n_zl, n_y, CAP, width)
        flat_rows = jnp.transpose(rows, (1, 2, 4, 5, 3, 0, 6)).reshape(
            n_x * n_zh * n_y * CAP, D
        )

    with jax.named_scope("experts"):
        pre_gate = jnp.dot(flat_rows, w_gate[0], preferred_element_type=jnp.float32)
        pre_up = jnp.dot(flat_rows, w_up[0], preferred_element_type=jnp.float32)
        hidden_units = (jax.nn.gelu(pre_gate) * pre_up).astype(jnp.bfloat16)
        projected = jnp.dot(hidden_units, w_down[0], preferred_element_type=jnp.float32).astype(
            jnp.bfloat16
        )

    with jax.named_scope("combine"):
        parts = projected.reshape(n_x, n_zh, n_y, CAP, n_zl, n_core, width)
        parts = jnp.transpose(parts, (5, 0, 1, 4, 2, 3, 6))
        parts = lax.psum_scatter(parts, "core", scatter_dimension=0, tiled=False)
        parts = lax.psum_scatter(parts, "x", scatter_dimension=0, tiled=False)
        parts = lax.psum_scatter(
            parts.reshape(n_zh * n_zl, n_y, CAP, width), ("zh", "zl"), scatter_dimension=0, tiled=False
        )
        outs = lax.all_to_all(parts, "y", split_axis=0, concat_axis=0, tiled=True)
        expert_cols = outs.reshape(EXPERTS * CAP, width).astype(jnp.float32)
        mixture = jnp.dot(combine[0], expert_cols, precision=lax.Precision.HIGHEST)
        layer_cols = (
            hidden_cols.astype(jnp.float32) + row_scale(mixture, col_slice(gain_post, width))
        ).astype(jnp.bfloat16)
        layer_out = lax.all_gather(layer_cols, CTX, axis=1, tiled=True)
    return layer_out[None]


def solution(mesh):
    n_exp = mesh.shape["exp"]
    n_ctx = mesh.shape["ctx"]
    sizes = {"y": EXPERTS, "x": n_exp // EXPERTS // 2, "zh": 2, "zl": n_ctx // 2, "core": 2}
    parts = {"exp": ("y", "x", "zh"), "ctx": ("zl", "core")}
    names = tuple(n for axis in mesh.axis_names for n in parts[axis])
    devices = np.asarray(mesh.devices).reshape(tuple(sizes[n] for n in names))
    fine = Mesh(devices, names)
    in_specs = (
        P(REQ, None, CTX),
        P(REQ, CTX, None),
        P(REQ, CTX, None),
        P(REQ, None, CTX),
        P(REQ, None, CTX),
        P(REQ, None),
        P(REQ, None, None),
        P(REQ, None, None),
        P(REQ, None, None),
        P(),
        P(),
        P(),
        P(REQ, None, CTX),
        P(REQ, None, CTX),
        P(REQ, CTX, None),
    )
    out_specs = P(REQ, None, None)
    return jax.shard_map(
        per_device, mesh=fine, in_specs=in_specs, out_specs=out_specs, check_vma=False
    )
```

time: 818 us -> 546 us (0.67)
  blocking collectives: 535 us -> 72.9 us
  local copies, waits for them, and re-layouts: 14.9 us -> 104 us
  waiting for transfers between devices: 202 us -> 289 us
  starting transfers between devices: 0.12 us -> 16.9 us
    all_to_all x2 -> x1, blocking collectives: 535 us -> 9.27 us  [per_device(): rows = lax.all_to_all(rows, 'y', split_axis=0, concat_axis=0, tiled=True)]
    reduce_scatter x0 -> x3, waiting for transfers between devices: none -> 137 us  [the longest x1 70.7 us: per_device(): parts = lax.psum_scatter(parts, 'x', scatter_dimension=0, tiled=False)]
    psum x1 -> x0, waiting for transfers between devices: 89.6 us -> none  [per_device(): expert_out = lax.psum(split_total, 'ctx')]
    reshape x0 -> x3, local copies, waits for them, and re-layouts: none -> 65.8 us  [the longest x2 39.4 us: per_device(): parts = projected.reshape(n_x, n_zh, n_y, CAP, n_zl, n_core, width)]
    psum x0 -> x3, blocking collectives: none -> 47.6 us  [row_scale(): lax.psum(jnp.sum(local_rows * local_rows, axis=-1, keepdims=True), CTX)]
    all_gather x3, waiting for transfers between devices: 111 us -> 141 us  [the longest x1 72.2 us: per_device(): rows = lax.all_gather(rows, 'x', axis=0, tiled=False)]
    transpose x0 -> x1, local copies, waits for them, and re-layouts: none -> 23.9 us  [per_device(): jnp.transpose(rows, (1, 2, 4, 5, 3, 0, 6))]
    all_to_all x0 -> x3, starting transfers between devices: none -> 16.5 us  [the longest x1 7.39 us: per_device(): lax.all_to_all(key_heads, CTX, split_axis=1, concat_axis=0, tiled=True)]
  transfers between devices with their start and end apart: 4 -> 9, of which waited for: 4 -> 8; matrix products, arithmetic and copies ran while one was open for 1% -> 3% of each run, Pallas kernels for 0% -> 0%
where the time goes in v1:
time: 546 us; the launch traced here: 544 us
  waiting for transfers between devices  289 us (53%)
  local copies, waits for them, and re-layouts  104 us (19%)
  blocking collectives  72.9 us (13%)
  matrix products  39.2 us (7%)
  starting transfers between devices  16.9 us (3%)
  between operations  13.6 us (2%)
  other arithmetic  7.93 us (1%)
    all_gather x1, waiting for transfers between devices, per_device(): rows = lax.all_gather(rows, 'x', axis=0, tiled=False)  72.2 us
    reduce_scatter x1, waiting for transfers between devices, per_device(): parts = lax.psum_scatter(parts, 'x', scatter_dimension=0, tiled=False)  70.7 us
    psum x3, blocking collectives, row_scale(): lax.psum(jnp.sum(local_rows * local_rows, axis=-1, keepdims=True), CTX)  47.6 us
    reshape x2, local copies, waits for them, and re-layouts, per_device(): parts = projected.reshape(n_x, n_zh, n_y, CAP, n_zl, n_core, width)  39.4 us
    reduce_scatter x1, waiting for transfers between devices, per_device(): lax.psum_scatter(parts.reshape(n_zh * n_zl, n_y, CAP, width), ('zh', 'zl'...  39 us
    all_gather x1, waiting for transfers between devices, per_device(): rows = lax.all_gather(rows, ('zh', 'zl'), axis=0, tiled=False)  35.6 us
    all_gather x1, waiting for transfers between devices, per_device(): rows = lax.all_gather(rows, 'core', axis=0, tiled=False)  33.2 us
    reduce_scatter x1, waiting for transfers between devices, per_device(): parts = lax.psum_scatter(parts, 'core', scatter_dimension=0, tiled=False)  27.3 us
  transfers between devices with their start and end apart: 9, of which 8 were waited for; matrix products, arithmetic and copies ran while one was open for 3% of the time, Pallas kernels for 0%

profile of v1, /device:TPU:1, one launch (start us, length us, event | category | flops | bytes accessed | tf_op | source)
XLA Modules:
  0.0 543.5 jit_solution(4893063763052339309)
XLA Ops:
  8.4 7.4 %all-to-all-start = ((bf16[128,8,128]{2,0,1:T(8,128)(2,1)}), bf16[128,8,128]{2,0,1:T(8,128)(2,1)S(1)}, u32[]{:S(2)}, u32[]{:S(2)}) async-start(bf16[128,8,128]{2,0,1:T(8,128)(2,1)} %copy.71), calls=%async_computation | async-start | bytes 524288 | tf_op jit(solution)/shard_map/attention/all_to_all | solution.py:100
  29.6 5.1 all-to-all-start.1
  34.7 2.4 convert_reduce_fusion
  37.2 6.3 %all-to-all-done.1 = bf16[128,8,128]{2,0,1:T(8,128)(2,1)} async-done(((bf16[128,8,128]{2,0,1:T(8,128)(2,1)}), bf16[128,8,128]{2,0,1:T(8,128)(2,1)}, u32[]{:S(2)}, u32[]{:S(2)}) %all-to-all-start.1) | async-done | bytes 262176 | tf_op jit(solution)/shard_map/attention/all_to_all | solution.py:101
  43.5 2.4 fusion.38
  45.9 14.0 %psum.21 = f32[64,1]{0,1:T(1,128)S(1)} all-reduce(f32[64,1]{0,1:T(1,128)S(1)} %bitcast.174), channel_id=1, replica_groups=mesh['zl'=4,'core'=2,'y'=4,'x'=4,'zh'=2] {'zl','core'}, use_global_device_ids=true, to_apply=%region_3.4 | all-reduce | flops 64 | bytes 512 | tf_op jit(solution)/shard_map/norms/psum | solution.py:65
  66.0 14.6 %psum.22 = f32[64,1]{0,1:T(1,128)S(1)} all-reduce(f32[64,1]{0,1:T(1,128)S(1)} %bitcast.172), channel_id=1, replica_groups=mesh['zl'=4,'core'=2,'y'=4,'x'=4,'zh'=2] {'zl','core'}, use_global_device_ids=true, to_apply=%region_9.10 | all-reduce | flops 64 | bytes 512 | tf_op jit(solution)/shard_map/norms/psum | solution.py:65
  81.9 9.3 %all_to_all.40 = bf16[4,32,768]{2,1,0:T(8,128)(2,1)} all-to-all(bf16[4,32,768]{2,1,0:T(8,128)(2,1)S(1)} %bitcast.171), channel_id=1, replica_groups=mesh['zl'=4,'core'=2,'y'=4,'x'=4,'zh'=2] {'y'}, dimensions={0} | all-to-all | bytes 393216 | tf_op jit(solution)/shard_map/dispatch/all_to_all | solution.py:132
  91.3 35.6 %all-gather.7.cloned.1.call-done = bf16[32,32,768]{2,1,0:T(8,128)(2,1)} async-done(((bf16[4,32,768]{2,1,0:T(8,128)(2,1)}), bf16[32,32,768]{2,1,0:T(8,128)(2,1)}) %all-gather.7.cloned.1.call-update) | async-done | bytes 1572880 | tf_op jit(solution)/shard_map/dispatch/all_gather | solution.py:133
  126.9 72.2 %all-gather.9.cloned.1.call-done = bf16[32,4,32,768]{3,2,1,0:T(8,128)(2,1)} async-done(((bf16[8,4,32,768]{3,2,1,0:T(8,128)(2,1)}), bf16[32,4,32,768]{3,2,1,0:T(8,128)(2,1)}) %all-gather.9.cloned.1.call-update) | async-done | bytes 6291472 | tf_op jit(solution)/shard_map/dispatch/all_gather | solution.py:134
  199.4 33.2 %all-gather.11.cloned.1.call-done = bf16[8,8,4,32,768]{4,3,2,1,0:T(8,128)(2,1)} async-done(((bf16[4,8,4,32,768]{4,3,2,1,0:T(8,128)(2,1)}), bf16[8,8,4,32,768]{4,3,2,1,0:T(8,128)(2,1)}) %all-gather.11.cloned.1.call-update) | async-done | bytes 12582928 | tf_op jit(solution)/shard_map/dispatch/all_gather | solution.py:135
  232.6 23.9 %copy.80 = bf16[4,2,4,32,4,2,768]{6,5,4,3,2,1,0:T(2,128)(2,1)} copy(bf16[4,2,4,32,4,2,768]{6,3,2,4,1,0,5:T(8,128)(2,1)} %bitcast.155) | data formatting | bytes 25165824 | tf_op jit(solution)/shard_map/dispatch/transpose | solution.py:140
  256.5 26.5 %reshape.423 = bf16[1024,6144]{1,0:T(8,128)(2,1)} reshape(bf16[4,2,4,32,4,2,768]{6,5,4,3,2,1,0:T(2,128)(2,1)} %copy.80) | data formatting | bytes 25165824 | tf_op jit(solution)/shard_map/dispatch/reshape | solution.py:140
  283.0 10.1 %fusion.26 = f32[1024,256]{1,0:T(8,128)} fusion(bf16[1024,6144]{1,0:T(8,128)(2,1)} %reshape.423, bf16[1,6144,256]{2,1,0:T(8,128)(2,1)} %param.27), kind=kOutput, calls=%fused_computation.28 | convolution fusion | flops 3223322624 | bytes 16777216 | tf_op jit(solution)/shard_map/experts/dot_general | solution.py:145
  293.0 19.8 %convolution_convert_fusion = bf16[1024,6144]{1,0:T(8,128)(2,1)} fusion(bf16[1,256,6144]{2,1,0:T(8,128)(2,1)S(1)} %copy-done, f32[1024,256]{1,0:T(8,128)} %fusion.26, bf16[1024,6144]{1,0:T(8,128)(2,1)} %reshape.423, bf16[1,6144,256]{2,1,0:T(8,128)(2,1)} %param.28), kind=kOutput, calls=%fused_computation.1 | convolution fusion | flops 6449266688 | bytes 32505856 | tf_op jit(solution)/shard_map/experts/dot_general | solution.py:148
  312.8 27.4 %reshape.424 = bf16[4,2,4,32,4,2,768]{6,5,4,3,2,1,0:T(2,128)(2,1)} reshape(bf16[1024,6144]{1,0:T(8,128)(2,1)} %convolution_convert_fusion) | data formatting | bytes 25165824 | tf_op jit(solution)/shard_map/combine/reshape | solution.py:153
  340.2 12.0 %copy.101 = bf16[4,2,4,32,4,2,768]{6,3,2,4,1,0,5:T(8,128)(2,1)} copy(bf16[4,2,4,32,4,2,768]{6,5,4,3,2,1,0:T(2,128)(2,1)} %reshape.424) | data formatting | bytes 25165824 | tf_op jit(solution)/shard_map/combine/reshape | solution.py:153
  352.3 27.3 %reduce-scatter.4.cloned.1.call-done = bf16[1,4,2,4,4,32,768]{6,5,4,3,2,1,0:T(8,128)(2,1)} async-done(((bf16[2,4,2,4,4,32,768]{6,5,4,3,2,1,0:T(8,128)(2,1)}), bf16[1,4,2,4,4,32,768]{6,5,4,3,2,1,0:T(8,128)(2,1)}) %reduce-scatter.4.cloned.1.call-update) | async-done | bytes 6291472 | tf_op jit(solution)/shard_map/combine/reduce_scatter | solution.py:155
  379.7 70.7 %reduce-scatter.6.cloned.1.call-done = bf16[1,2,4,4,32,768]{5,4,3,2,1,0:T(8,128)(2,1)} async-done(((bf16[4,2,4,4,32,768]{5,4,3,2,1,0:T(8,128)(2,1)}), bf16[1,2,4,4,32,768]{5,4,3,2,1,0:T(8,128)(2,1)}) %reduce-scatter.6.cloned.1.call-update) | async-done | bytes 1572880 | tf_op jit(solution)/shard_map/combine/reduce_scatter | solution.py:156
  450.4 39.0 %reduce-scatter.8.cloned.1.call-done = bf16[1,4,32,768]{3,2,1,0:T(8,128)(2,1)} async-done(((bf16[8,4,32,768]{3,2,1,0:T(8,128)(2,1)}), bf16[1,4,32,768]{3,2,1,0:T(8,128)(2,1)}) %reduce-scatter.8.cloned.1.call-update) | async-done | bytes 196624 | tf_op jit(solution)/shard_map/combine/reduce_scatter | solution.py:157
  489.4 4.0 all-to-all-start.3
  494.2 4.4 all-to-all-done.3
  499.7 19.0 %psum.23 = f32[64,1]{0,1:T(1,128)S(1)} all-reduce(f32[64,1]{0,1:T(1,128)S(1)} %bitcast.173), channel_id=1, replica_groups=mesh['zl'=4,'core'=2,'y'=4,'x'=4,'zh'=2] {'zl','core'}, use_global_device_ids=true, to_apply=%region_14.15 | all-reduce | flops 64 | bytes 512 | tf_op jit(solution)/shard_map/combine/psum | solution.py:65
  519.7 16.1 %all_gather.27 = bf16[64,6144]{1,0:T(8,128)(2,1)S(1)} all-gather(bf16[64,768]{1,0:T(8,128)(2,1)S(1)} %fusion.31), channel_id=1, replica_groups=mesh['zl'=4,'core'=2,'y'=4,'x'=4,'zh'=2] {'zl','core'}, dimensions={1}, use_global_device_ids=true | all-gather | bytes 884736 | tf_op jit(solution)/shard_map/combine/all_gather | solution.py:166
  (58 shorter events, 27.4 us)
Async XLA Ops:
  6.5 286.5 %copy-start = (bf16[1,256,6144]{2,1,0:T(8,128)(2,1)S(1)}, bf16[1,256,6144]{2,1,0:T(8,128)(2,1)}, u32[]{:S(2)}) copy-start(bf16[1,256,6144]{2,1,0:T(8,128)(2,1)} %param.29) | copy-start | bytes 9437188
  6.5 22.2 %copy-start.2 = (bf16[1,64,128]{2,1,0:T(8,128)(2,1)S(1)}, bf16[1,64,128]{2,1,0:T(8,128)(2,1)}, u32[]{:S(2)}) copy-start(bf16[1,64,128]{2,1,0:T(8,128)(2,1)} %param.19) | copy-start | bytes 49156
  8.4 21.2 %all-to-all-start = ((bf16[128,8,128]{2,0,1:T(8,128)(2,1)}), bf16[128,8,128]{2,0,1:T(8,128)(2,1)S(1)}, u32[]{:S(2)}, u32[]{:S(2)}) async-start(bf16[128,8,128]{2,0,1:T(8,128)(2,1)} %copy.71), calls=%async_computation | async-start | bytes 524288 | tf_op jit(solution)/shard_map/attention/all_to_all | solution.py:100
  19.7 0.5 copy-start.3
  29.6 13.9 %all-to-all-start.1 = ((bf16[128,8,128]{2,0,1:T(8,128)(2,1)}), bf16[128,8,128]{2,0,1:T(8,128)(2,1)}, u32[]{:S(2)}, u32[]{:S(2)}) async-start(bf16[128,8,128]{2,0,1:T(8,128)(2,1)} %copy.73), calls=%async_computation.1 | async-start | bytes 524288 | tf_op jit(solution)/shard_map/attention/all_to_all | solution.py:101
  34.7 92.2 %all-gather.7.cloned.1.call-start = ((), (), s32[]{:S(2)}) async-start(), calls=%async_computation.10 | async-start | bytes 1769472 | tf_op jit(solution)/shard_map/dispatch/all_gather | solution.py:133
  91.2 107.9 %all-gather.9.cloned.1.call-start = ((), (), s32[]{:S(2)}) async-start(), calls=%async_computation.11 | async-start | bytes 7864320 | tf_op jit(solution)/shard_map/dispatch/all_gather | solution.py:134
  126.9 105.7 %all-gather.11.cloned.1.call-start = ((), (), s32[]{:S(2)}) async-start(), calls=%async_computation.12 | async-start | bytes 18874368 | tf_op jit(solution)/shard_map/dispatch/all_gather | solution.py:135
  199.1 180.4 %reduce-scatter.4.cloned.1.call-start = ((), (), s32[]{:S(2)}) async-start(), calls=%async_computation.7 | async-start | bytes 18874368 | tf_op jit(solution)/shard_map/combine/reduce_scatter | solution.py:155
  352.2 98.2 %reduce-scatter.6.cloned.1.call-start = ((), (), s32[]{:S(2)}) async-start(), calls=%async_computation.8 | async-start | bytes 7864320 | tf_op jit(solution)/shard_map/combine/reduce_scatter | solution.py:156
  379.6 157.1 %copy-start.1 = (bf16[1,256,6144]{2,1,0:T(8,128)(2,1)S(1)}, bf16[1,256,6144]{2,1,0:T(8,128)(2,1)}, u32[]{:S(2)}) copy-start(bf16[1,256,6144]{2,1,0:T(8,128)(2,1)} %param.29) | copy-start | bytes 9437188
  379.6 109.8 %reduce-scatter.8.cloned.1.call-start = ((), (), s32[]{:S(2)}) async-start(), calls=%async_computation.9 | async-start | bytes 1769472 | tf_op jit(solution)/shard_map/combine/reduce_scatter | solution.py:157
  489.4 9.2 %all-to-all-start.3 = ((bf16[4,32,768]{2,1,0:T(8,128)(2,1)}), bf16[4,32,768]{2,1,0:T(8,128)(2,1)S(1)}, u32[]{:S(2)}, u32[]{:S(2)}) async-start(bf16[4,32,768]{2,1,0:T(8,128)(2,1)} %bitcast.170), calls=%async_computation.6 | async-start | bytes 393216 | tf_op jit(solution)/shard_map/combine/all_to_all | solution.py:160
Sparse Core Ops, SparseCore 0:
  91.3 35.4 all-gather.6
  128.7 70.4 all-gather.8
  200.9 31.5 all-gather.10
  352.3 27.1 reduce-scatter.3
  382.0 68.3 reduce-scatter.5
  452.8 36.5 reduce-scatter.7

commit v2 on v1

--- a/solution.py
+++ b/solution.py
@@ -121,6 +121,9 @@
         )
 
     dispatch, combine = route_tables(expert_ids, gate_num)
+    n_zl = D // width // 2
+    group = CAP // n_zl
+    swap = [(0, 1), (1, 0)]
     with jax.named_scope("dispatch"):
         buffer = jnp.einsum(
             "ns,nd->sd",
@@ -128,36 +131,54 @@
             normed_cols,
             preferred_element_type=jnp.float32,
         ).astype(jnp.bfloat16)
-        rows = buffer.reshape(EXPERTS, CAP, width)
+        rows = buffer.reshape(EXPERTS, n_zl, group, 1, width)
+        rows = lax.all_to_all(rows, "zl", split_axis=1, concat_axis=3, tiled=True)
+        rows = rows.reshape(EXPERTS, group, n_zl, width)
         rows = lax.all_to_all(rows, "y", split_axis=0, concat_axis=0, tiled=True)
-        rows = lax.all_gather(rows, ("zh", "zl"), axis=0, tiled=False)
-        rows = lax.all_gather(rows, "x", axis=0, tiled=False)
-        rows = lax.all_gather(rows, "core", axis=0, tiled=False)
-        n_core, n_x, n_z, n_y = rows.shape[:4]
-        n_zh = 2
-        n_zl = n_z // n_zh
-        rows = rows.reshape(n_core, n_x, n_zh, n_zl, n_y, CAP, width)
-        flat_rows = jnp.transpose(rows, (1, 2, 4, 5, 3, 0, 6)).reshape(
-            n_x * n_zh * n_y * CAP, D
-        )
+        rows = lax.all_gather(rows, ("zh", "zl"), axis=0, tiled=True)
+        rows = lax.all_gather(rows, "x", axis=0, tiled=True)
+        own_rows = rows.reshape(-1, n_zl * width)
+        other_rows = lax.ppermute(own_rows, "core", swap)
 
     with jax.named_scope("experts"):
-        pre_gate = jnp.dot(flat_rows, w_gate[0], preferred_element_type=jnp.float32)
-        pre_up = jnp.dot(flat_rows, w_up[0], preferred_element_type=jnp.float32)
+        core = lax.axis_index("core")
+
+        def halves(mat, axis):
+            shape = mat.shape
+            split = shape[:axis] + (n_zl, 2, width) + shape[axis + 1 :]
+            mat = mat.reshape(split)
+            own = lax.dynamic_index_in_dim(mat, core, axis + 1, keepdims=False)
+            other = lax.dynamic_index_in_dim(mat, 1 - core, axis + 1, keepdims=False)
+            merged = shape[:axis] + (n_zl * width,) + shape[axis + 1 :]
+            return own.reshape(merged), other.reshape(merged)
+
+        gate_own, gate_other = halves(w_gate[0], 0)
+        up_own, up_other = halves(w_up[0], 0)
+        down_own, down_other = halves(w_down[0], 1)
+        pre_gate = jnp.dot(own_rows, gate_own, preferred_element_type=jnp.float32) + jnp.dot(
+            other_rows, gate_other, preferred_element_type=jnp.float32
+        )
+        pre_up = jnp.dot(own_rows, up_own, preferred_element_type=jnp.float32) + jnp.dot(
+            other_rows, up_other, preferred_element_type=jnp.float32
+        )
         hidden_units = (jax.nn.gelu(pre_gate) * pre_up).astype(jnp.bfloat16)
-        projected = jnp.dot(hidden_units, w_down[0], preferred_element_type=jnp.float32).astype(
+        piece_own = jnp.dot(hidden_units, down_own, preferred_element_type=jnp.float32).astype(
             jnp.bfloat16
         )
+        piece_other = jnp.dot(
+            hidden_units, down_other, preferred_element_type=jnp.float32
+        ).astype(jnp.bfloat16)
 
     with jax.named_scope("combine"):
-        parts = projected.reshape(n_x, n_zh, n_y, CAP, n_zl, n_core, width)
-        parts = jnp.transpose(parts, (5, 0, 1, 4, 2, 3, 6))
-        parts = lax.psum_scatter(parts, "core", scatter_dimension=0, tiled=False)
-        parts = lax.psum_scatter(parts, "x", scatter_dimension=0, tiled=False)
-        parts = lax.psum_scatter(
-            parts.reshape(n_zh * n_zl, n_y, CAP, width), ("zh", "zl"), scatter_dimension=0, tiled=False
-        )
+        received = lax.ppermute(piece_other, "core", swap)
+        parts = (piece_own.astype(jnp.float32) + received.astype(jnp.float32)).astype(jnp.bfloat16)
+        parts = parts.reshape(rows.shape)
+        parts = lax.psum_scatter(parts, "x", scatter_dimension=0, tiled=True)
+        parts = parts.reshape((2 * n_zl, -1) + parts.shape[1:])
+        parts = lax.psum_scatter(parts, ("zh", "zl"), scatter_dimension=0, tiled=False)
         outs = lax.all_to_all(parts, "y", split_axis=0, concat_axis=0, tiled=True)
+        outs = outs.reshape(EXPERTS, 1, group, n_zl, width)
+        outs = lax.all_to_all(outs, "zl", split_axis=3, concat_axis=1, tiled=True)
         expert_cols = outs.reshape(EXPERTS * CAP, width).astype(jnp.float32)
         mixture = jnp.dot(combine[0], expert_cols, precision=lax.Precision.HIGHEST)
         layer_cols = (

time: 546 us -> 405 us (0.74)
  local copies, waits for them, and re-layouts: 104 us -> 15.6 us
  waiting for transfers between devices: 289 us -> 242 us
  blocking collectives: 72.9 us -> 92.3 us
  matrix products: 39.2 us -> 22.3 us
  other arithmetic: 7.93 us -> 1.88 us
    reshape x3, local copies, waits for them, and re-layouts: 65.8 us -> 0.72 us  [the longest x1 0.69 us: per_device(): outs = outs.reshape(EXPERTS, 1, group, n_zl, width)]
    all_gather x3 -> x2, waiting for transfers between devices: 141 us -> 109 us  [the longest x1 72.2 us: per_device(): rows = lax.all_gather(rows, 'x', axis=0, tiled=True)]
    reduce_scatter x3 -> x2, waiting for transfers between devices: 137 us -> 106 us  [the longest x1 66.7 us: per_device(): parts = lax.psum_scatter(parts, 'x', scatter_dimension=0, tiled=True)]
    transpose x1 -> x0, local copies, waits for them, and re-layouts: 23.9 us -> none  [per_device(): jnp.transpose(rows, (1, 2, 4, 5, 3, 0, 6))]
    all_to_all x0 -> x2, blocking collectives: none -> 17.6 us  [the longest x1 9.18 us: per_device(): outs = lax.all_to_all(parts, 'y', split_axis=0, concat_axis=0, tiled=True)]
    dot_general x2 -> x6, matrix products: 29.9 us -> 19.2 us  [the longest x1 4.73 us: per_device(): jnp.dot(other_rows, gate_other, preferred_element_type=jnp.float32)]
    ppermute x0 -> x2, waiting for transfers between devices: none -> 10.1 us  [the longest x1 10.1 us: per_device(): received = lax.ppermute(piece_other, 'core', swap)]
where the time goes in v2:
time: 405 us; the launch traced here: 404 us
  waiting for transfers between devices  242 us (60%)
  blocking collectives  92.3 us (23%)
  matrix products  22.3 us (6%)
  starting transfers between devices  16.3 us (4%)
  local copies, waits for them, and re-layouts  15.6 us (4%)
  between operations  13.5 us (3%)
    all_gather x1, waiting for transfers between devices, per_device(): rows = lax.all_gather(rows, 'x', axis=0, tiled=True)  72.2 us
    reduce_scatter x1, waiting for transfers between devices, per_device(): parts = lax.psum_scatter(parts, 'x', scatter_dimension=0, tiled=True)  66.7 us
    psum x3, blocking collectives, row_scale(): lax.psum(jnp.sum(local_rows * local_rows, axis=-1, keepdims=True), CTX)  49.3 us
    reduce_scatter x1, waiting for transfers between devices, per_device(): lax.psum_scatter(parts, ('zh', 'zl'), scatter_dimension=0, tiled=False)  39 us
    all_gather x1, waiting for transfers between devices, per_device(): rows = lax.all_gather(rows, ('zh', 'zl'), axis=0, tiled=True)  37.3 us
    all_gather x1, blocking collectives, per_device(): layer_out = lax.all_gather(layer_cols, CTX, axis=1, tiled=True)  16.1 us
    ppermute x1, waiting for transfers between devices, per_device(): received = lax.ppermute(piece_other, 'core', swap)  10.1 us
    unnamed x30, local copies, waits for them, and re-layouts  9.54 us
  transfers between devices with their start and end apart: 9, of which 8 were waited for; matrix products, arithmetic and copies ran while one was open for 3% of the time, Pallas kernels for 0%

profile of v2, /device:TPU:1, one launch (start us, length us, event | category | flops | bytes accessed | tf_op | source)
XLA Modules:
  0.0 404.2 jit_solution(4442463963612626807)
XLA Ops:
  8.4 7.4 %all-to-all-start = ((bf16[128,8,128]{2,0,1:T(8,128)(2,1)}), bf16[128,8,128]{2,0,1:T(8,128)(2,1)S(1)}, u32[]{:S(2)}, u32[]{:S(2)}) async-start(bf16[128,8,128]{2,0,1:T(8,128)(2,1)} %copy.106), calls=%async_computation | async-start | bytes 524288 | tf_op jit(solution)/shard_map/attention/all_to_all | solution.py:100
  19.9 4.6 %all-to-all-done = bf16[128,8,128]{2,0,1:T(8,128)(2,1)S(1)} async-done(((bf16[128,8,128]{2,0,1:T(8,128)(2,1)}), bf16[128,8,128]{2,0,1:T(8,128)(2,1)S(1)}, u32[]{:S(2)}, u32[]{:S(2)}) %all-to-all-start) | async-done | bytes 262176 | tf_op jit(solution)/shard_map/attention/all_to_all | solution.py:100
  24.5 4.4 %all-to-all-start.1 = ((bf16[128,8,128]{2,0,1:T(8,128)(2,1)}), bf16[128,8,128]{2,0,1:T(8,128)(2,1)S(1)}, u32[]{:S(2)}, u32[]{:S(2)}) async-start(bf16[128,8,128]{2,0,1:T(8,128)(2,1)} %copy.108), calls=%async_computation.1 | async-start | bytes 524288 | tf_op jit(solution)/shard_map/attention/all_to_all | solution.py:101
  29.6 7.9 %all-to-all-done.1 = bf16[128,8,128]{2,0,1:T(8,128)(2,1)S(1)} async-done(((bf16[128,8,128]{2,0,1:T(8,128)(2,1)}), bf16[128,8,128]{2,0,1:T(8,128)(2,1)S(1)}, u32[]{:S(2)}, u32[]{:S(2)}) %all-to-all-start.1) | async-done | bytes 262176 | tf_op jit(solution)/shard_map/attention/all_to_all | solution.py:101
  38.0 14.0 %psum.21 = f32[64,1]{0,1:T(1,128)S(1)} all-reduce(f32[64,1]{0,1:T(1,128)S(1)} %bitcast.192), channel_id=1, replica_groups=mesh['zl'=4,'core'=2,'y'=4,'x'=4,'zh'=2] {'zl','core'}, use_global_device_ids=true, to_apply=%region_3.4 | all-reduce | flops 64 | bytes 512 | tf_op jit(solution)/shard_map/norms/psum | solution.py:65
  53.5 14.5 %psum.22 = f32[64,1]{0,1:T(1,128)S(1)} all-reduce(f32[64,1]{0,1:T(1,128)S(1)} %bitcast.185), channel_id=1, replica_groups=mesh['zl'=4,'core'=2,'y'=4,'x'=4,'zh'=2] {'zl','core'}, use_global_device_ids=true, to_apply=%region_9.10 | all-reduce | flops 64 | bytes 512 | tf_op jit(solution)/shard_map/norms/psum | solution.py:65
  69.3 8.5 %all_to_all.70 = bf16[4,4,8,1,768]{4,2,0,3,1:T(8,128)(2,1)S(1)} all-to-all(bf16[4,4,8,1,768]{4,2,0,3,1:T(8,128)(2,1)S(1)} %copy.115), channel_id=1, replica_groups=mesh['zl'=4,'core'=2,'y'=4,'x'=4,'zh'=2] {'zl'}, dimensions={1} | all-to-all | bytes 393216 | tf_op jit(solution)/shard_map/dispatch/all_to_all | solution.py:135
  77.7 9.3 %all_to_all.71 = bf16[4,8,4,768]{3,1,2,0:T(8,128)(2,1)} all-to-all(bf16[4,8,4,768]{3,1,2,0:T(8,128)(2,1)S(1)} %copy.116), channel_id=1, replica_groups=mesh['zl'=4,'core'=2,'y'=4,'x'=4,'zh'=2] {'y'}, dimensions={0} | all-to-all | bytes 393216 | tf_op jit(solution)/shard_map/dispatch/all_to_all | solution.py:137
  87.1 37.3 %all-gather.3.cloned.1.call-done = bf16[32,8,4,768]{3,1,2,0:T(8,128)(2,1)} async-done(((bf16[4,8,4,768]{3,1,2,0:T(8,128)(2,1)}), bf16[32,8,4,768]{3,1,2,0:T(8,128)(2,1)}) %all-gather.3.cloned.1.call-update) | async-done | bytes 1572880 | tf_op jit(solution)/shard_map/dispatch/all_gather | solution.py:138
  124.4 72.2 %all-gather.5.cloned.1.call-done = bf16[128,8,4,768]{3,1,2,0:T(8,128)(2,1)} async-done(((bf16[32,8,4,768]{3,1,2,0:T(8,128)(2,1)}), bf16[128,8,4,768]{3,1,2,0:T(8,128)(2,1)}) %all-gather.5.cloned.1.call-update) | async-done | bytes 6291472 | tf_op jit(solution)/shard_map/dispatch/all_gather | solution.py:139
  197.5 3.2 copy.117
  205.5 1.8 fusion.43
  209.1 4.7 %fusion.15 = f32[1024,256]{1,0:T(8,128)S(1)} fusion(f32[1024,256]{1,0:T(8,128)S(1)} %fusion.43, bf16[1024,3072]{1,0:T(8,128)(2,1)} %collective-permute-done, bf16[3072,256]{1,0:T(8,128)(2,1)S(1)} %bitcast.169), kind=kOutput, calls=%fused_computation.25 | convolution fusion | flops 1612972032 | bytes 9961472 | tf_op jit(solution)/shard_map/experts/dot_general | solution.py:158
  213.9 4.6 %fusion.2 = bf16[1024,256]{1,0:T(8,128)(2,1)S(1)} fusion(f32[1024,256]{1,0:T(8,128)S(1)} %fusion.15, f32[1024,256]{1,0:T(8,128)S(1)} %fusion.44, bf16[1024,3072]{1,0:T(8,128)(2,1)} %collective-permute-done, bf16[3072,256]{1,0:T(8,128)(2,1)S(1)} %bitcast.168), kind=kOutput, calls=%fused_computation.9 | convolution fusion | flops 1611399168 | bytes 10485760 | tf_op jit(solution)/shard_map/experts/dot_general | solution.py:161
  218.5 1.8 convolution_convert_fusion
  220.4 10.1 %collective-permute-done.1 = bf16[1024,3072]{1,0:T(8,128)(2,1)S(1)} collective-permute-done((bf16[1024,3072]{1,0:T(8,128)(2,1)S(1)}, bf16[1024,3072]{1,0:T(8,128)(2,1)S(1)}, u32[]{:S(2)}, u32[]{:S(2)}) %collective-permute-start.1) | collective-permute-done | bytes 6291488 | tf_op jit(solution)/shard_map/combine/ppermute | solution.py:173
  230.6 4.5 %add_convert_fusion = bf16[1024,3072]{1,0:T(8,128)(2,1)} fusion(bf16[1024,3072]{1,0:T(8,128)(2,1)S(1)} %collective-permute-done.1, bf16[1024,256]{1,0:T(8,128)(2,1)S(1)} %fusion.2, bf16[256,3072]{0,1:T(8,128)(2,1)S(1)} %bitcast.161), kind=kOutput, calls=%fused_computation | convolution fusion | flops 1626341376 | bytes 14680064 | tf_op jit(solution)/shard_map/experts/dot_general | solution.py:165
  235.1 66.7 %reduce-scatter.3.cloned.1.call-done = bf16[32,8,4,768]{3,1,2,0:T(8,128)(2,1)} async-done(((bf16[128,8,4,768]{3,1,2,0:T(8,128)(2,1)}), bf16[32,8,4,768]{3,1,2,0:T(8,128)(2,1)}) %reduce-scatter.3.cloned.1.call-update) | async-done | bytes 1572880 | tf_op jit(solution)/shard_map/combine/reduce_scatter | solution.py:176
  301.9 39.0 %reduce-scatter.5.cloned.1.call-done = bf16[1,4,8,4,768]{4,2,3,1,0:T(8,128)(2,1)} async-done(((bf16[8,4,8,4,768]{4,2,3,1,0:T(8,128)(2,1)}), bf16[1,4,8,4,768]{4,2,3,1,0:T(8,128)(2,1)}) %reduce-scatter.5.cloned.1.call-update) | async-done | bytes 196624 | tf_op jit(solution)/shard_map/combine/reduce_scatter | solution.py:178
  340.9 9.2 %all_to_all.72 = bf16[4,8,4,768]{3,1,2,0:T(8,128)(2,1)S(1)} all-to-all(bf16[4,8,4,768]{3,1,2,0:T(8,128)(2,1)} %bitcast.183), channel_id=1, replica_groups=mesh['zl'=4,'core'=2,'y'=4,'x'=4,'zh'=2] {'y'}, dimensions={0} | all-to-all | bytes 393216 | tf_op jit(solution)/shard_map/combine/all_to_all | solution.py:179
  350.8 3.5 all-to-all-start.5
  355.0 4.3 %all-to-all-done.5 = bf16[4,1,8,4,768]{4,2,0,1,3:T(8,128)(2,1)S(1)} async-done(((bf16[4,1,8,4,768]{4,2,0,1,3:T(8,128)(2,1)}), bf16[4,1,8,4,768]{4,2,0,1,3:T(8,128)(2,1)S(1)}, u32[]{:S(2)}, u32[]{:S(2)}) %all-to-all-start.5) | async-done | bytes 196640 | tf_op jit(solution)/shard_map/combine/all_to_all | solution.py:181
  359.7 20.8 %psum.23 = f32[64,1]{0,1:T(1,128)S(1)} all-reduce(f32[64,1]{0,1:T(1,128)S(1)} %bitcast.186), channel_id=1, replica_groups=mesh['zl'=4,'core'=2,'y'=4,'x'=4,'zh'=2] {'zl','core'}, use_global_device_ids=true, to_apply=%region_13.14 | all-reduce | flops 64 | bytes 512 | tf_op jit(solution)/shard_map/combine/psum | solution.py:65
  380.6 16.1 %all_gather.11 = bf16[64,6144]{1,0:T(8,128)(2,1)S(1)} all-gather(bf16[64,768]{1,0:T(8,128)(2,1)S(1)} %fusion.18), channel_id=1, replica_groups=mesh['zl'=4,'core'=2,'y'=4,'x'=4,'zh'=2] {'zl','core'}, dimensions={1}, use_global_device_ids=true | all-gather | bytes 884736 | tf_op jit(solution)/shard_map/combine/all_gather | solution.py:187
  (82 shorter events, 20.3 us)
Async XLA Ops:
  6.5 13.2 %copy-start = (bf16[1,64,128]{2,1,0:T(8,128)(2,1)S(1)}, bf16[1,64,128]{2,1,0:T(8,128)(2,1)}, u32[]{:S(2)}) copy-start(bf16[1,64,128]{2,1,0:T(8,128)(2,1)} %param.19) | copy-start | bytes 49156
  6.5 9.3 %copy-start.5 = (bf16[1,64,768]{2,1,0:T(8,128)(2,1)S(1)}, bf16[1,64,768]{2,1,0:T(8,128)(2,1)}, u32[]{:S(2)}) copy-start(bf16[1,64,768]{2,1,0:T(8,128)(2,1)} %param.15) | copy-start | bytes 294916
  6.5 9.4 %copy-start.9 = (s32[1,64]{1,0:T(1,128)S(1)}, s32[1,64]{1,0:T(1,128)}, u32[]{:S(2)}) copy-start(s32[1,64]{1,0:T(1,128)} %param.20) | copy-start | bytes 772
  6.5 9.5 %copy-start.6 = (s32[1,64,2]{1,2,0:T(2,128)S(1)}, s32[1,64,2]{1,2,0:T(2,128)}, u32[]{:S(2)}) copy-start(s32[1,64,2]{1,2,0:T(2,128)} %param.22) | copy-start | bytes 1540
  6.5 10.4 %copy-start.7 = (s32[1,64,2]{1,2,0:T(2,128)S(1)}, s32[1,64,2]{1,2,0:T(2,128)}, u32[]{:S(2)}) copy-start(s32[1,64,2]{1,2,0:T(2,128)} %param.23) | copy-start | bytes 1540
  6.5 10.4 %copy-start.8 = (bf16[1,64,128]{2,1,0:T(8,128)(2,1)S(1)}, bf16[1,64,128]{2,1,0:T(8,128)(2,1)}, u32[]{:S(2)}) copy-start(bf16[1,64,128]{2,1,0:T(8,128)(2,1)} %param.18) | copy-start | bytes 49156
  6.6 10.8 %copy-start.4 = (bf16[1,128,1024]{2,1,0:T(8,128)(2,1)S(1)}, bf16[1,128,1024]{2,1,0:T(8,128)(2,1)}, u32[]{:S(2)}) copy-start(bf16[1,128,1024]{2,1,0:T(8,128)(2,1)} %param.17) | copy-start | bytes 786436
  8.4 16.1 %all-to-all-start = ((bf16[128,8,128]{2,0,1:T(8,128)(2,1)}), bf16[128,8,128]{2,0,1:T(8,128)(2,1)S(1)}, u32[]{:S(2)}, u32[]{:S(2)}) async-start(bf16[128,8,128]{2,0,1:T(8,128)(2,1)} %copy.106), calls=%async_computation | async-start | bytes 524288 | tf_op jit(solution)/shard_map/attention/all_to_all | solution.py:100
  24.5 13.1 %all-to-all-start.1 = ((bf16[128,8,128]{2,0,1:T(8,128)(2,1)}), bf16[128,8,128]{2,0,1:T(8,128)(2,1)S(1)}, u32[]{:S(2)}, u32[]{:S(2)}) async-start(bf16[128,8,128]{2,0,1:T(8,128)(2,1)} %copy.108), calls=%async_computation.1 | async-start | bytes 524288 | tf_op jit(solution)/shard_map/attention/all_to_all | solution.py:101
  28.8 95.5 %all-gather.3.cloned.1.call-start = ((), (), s32[]{:S(2)}) async-start(), calls=%async_computation.8 | async-start | bytes 1769472 | tf_op jit(solution)/shard_map/dispatch/all_gather | solution.py:138
  87.0 109.6 %all-gather.5.cloned.1.call-start = ((), (), s32[]{:S(2)}) async-start(), calls=%async_computation.9 | async-start | bytes 7864320 | tf_op jit(solution)/shard_map/dispatch/all_gather | solution.py:139
  124.4 177.4 %reduce-scatter.3.cloned.1.call-start = ((), (), s32[]{:S(2)}) async-start(), calls=%async_computation.10 | async-start | bytes 7864320 | tf_op jit(solution)/shard_map/combine/reduce_scatter | solution.py:176
  196.6 12.5 %collective-permute-start = (bf16[1024,3072]{1,0:T(8,128)(2,1)}, bf16[1024,3072]{1,0:T(8,128)(2,1)}, u32[]{:S(2)}, u32[]{:S(2)}) collective-permute-start(bf16[1024,3072]{1,0:T(8,128)(2,1)} %bitcast.187), channel_id=1, source_target_pairs={{0,32},{32,0},{1,33},{33,1},{2,34},{34,2},{3,35},{35,3},{4,36},{36... | collective-permute-start | bytes 18874376 | tf_op jit(solution)/shard_map/dispatch/ppermute | solution.py:141
  200.6 1.9 copy-start.2
  200.7 2.8 copy-start.3
  200.7 4.0 slice-start
  203.5 2.0 slice-start.1
  220.3 10.2 %collective-permute-start.1 = (bf16[1024,3072]{1,0:T(8,128)(2,1)S(1)}, bf16[1024,3072]{1,0:T(8,128)(2,1)S(1)}, u32[]{:S(2)}, u32[]{:S(2)}) collective-permute-start(bf16[1024,3072]{1,0:T(8,128)(2,1)S(1)} %convolution_convert_fusion), channel_id=1, source_target_pairs={{0,32},{32,0},{1,33},{33,1},{2,34},{34,2},{3,35},{35,3},{4,36},{36... | collective-permute-start | bytes 18874376 | tf_op jit(solution)/shard_map/combine/ppermute | solution.py:173
  235.1 105.8 %reduce-scatter.5.cloned.1.call-start = ((), (), s32[]{:S(2)}) async-start(), calls=%async_computation.11 | async-start | bytes 1769472 | tf_op jit(solution)/shard_map/combine/reduce_scatter | solution.py:178
  350.8 8.6 %all-to-all-start.5 = ((bf16[4,1,8,4,768]{4,2,0,1,3:T(8,128)(2,1)}), bf16[4,1,8,4,768]{4,2,0,1,3:T(8,128)(2,1)S(1)}, u32[]{:S(2)}, u32[]{:S(2)}) async-start(bf16[4,1,8,4,768]{4,2,0,1,3:T(8,128)(2,1)} %copy.118), calls=%async_computation.7 | async-start | bytes 393216 | tf_op jit(solution)/shard_map/combine/all_to_all | solution.py:181
  359.4 38.2 %copy-start.1 = (bf16[1,64,128]{2,1,0:T(8,128)(2,1)S(1)}, bf16[1,64,128]{2,1,0:T(8,128)(2,1)}, u32[]{:S(2)}) copy-start(bf16[1,64,128]{2,1,0:T(8,128)(2,1)} %param.19) | copy-start | bytes 49156
Sparse Core Ops, SparseCore 0:
  87.1 37.1 all-gather.2
  126.2 70.4 all-gather.4
  235.2 66.6 reduce-scatter.2
  304.3 36.5 reduce-scatter.4

commit v3 on v2

--- a/solution.py
+++ b/solution.py
@@ -95,12 +95,12 @@
             query_row_block, query_slot, fresh_keys[0], fresh_values[0], query_slot
         )
         cache_rows = cached_keys.shape[1]
-        key_heads = cached_keys[0].reshape(cache_rows, n_ctx, head_width)
-        value_heads = cached_values[0].reshape(cache_rows, n_ctx, head_width)
-        key_part = lax.all_to_all(key_heads, CTX, split_axis=1, concat_axis=0, tiled=True)
-        value_part = lax.all_to_all(value_heads, CTX, split_axis=1, concat_axis=0, tiled=True)
-        key_part = key_part.reshape(-1, head_width)
-        value_part = value_part.reshape(-1, head_width)
+        both_heads = jnp.stack([cached_keys[0], cached_values[0]]).reshape(
+            2, cache_rows, n_ctx, head_width
+        )
+        both_part = lax.all_to_all(both_heads, CTX, split_axis=2, concat_axis=1, tiled=True)
+        key_part = both_part[0].reshape(-1, head_width)
+        value_part = both_part[1].reshape(-1, head_width)
         cache_slot = jnp.full((key_part.shape[0],), -1.0, jnp.float32)
         numer_part, total_part = attend_part(
             query_row_block, query_slot, key_part, value_part, cache_slot
@@ -131,10 +131,9 @@
             normed_cols,
             preferred_element_type=jnp.float32,
         ).astype(jnp.bfloat16)
-        rows = buffer.reshape(EXPERTS, n_zl, group, 1, width)
-        rows = lax.all_to_all(rows, "zl", split_axis=1, concat_axis=3, tiled=True)
-        rows = rows.reshape(EXPERTS, group, n_zl, width)
-        rows = lax.all_to_all(rows, "y", split_axis=0, concat_axis=0, tiled=True)
+        rows = buffer.reshape(EXPERTS * n_zl, group, width)
+        rows = lax.all_to_all(rows, ("y", "zl"), split_axis=0, concat_axis=0, tiled=True)
+        rows = jnp.transpose(rows.reshape(EXPERTS, n_zl, group, width), (0, 2, 1, 3))
         rows = lax.all_gather(rows, ("zh", "zl"), axis=0, tiled=True)
         rows = lax.all_gather(rows, "x", axis=0, tiled=True)
         own_rows = rows.reshape(-1, n_zl * width)
@@ -176,9 +175,9 @@
         parts = lax.psum_scatter(parts, "x", scatter_dimension=0, tiled=True)
         parts = parts.reshape((2 * n_zl, -1) + parts.shape[1:])
         parts = lax.psum_scatter(parts, ("zh", "zl"), scatter_dimension=0, tiled=False)
-        outs = lax.all_to_all(parts, "y", split_axis=0, concat_axis=0, tiled=True)
-        outs = outs.reshape(EXPERTS, 1, group, n_zl, width)
-        outs = lax.all_to_all(outs, "zl", split_axis=3, concat_axis=1, tiled=True)
+        parts = jnp.transpose(parts.reshape(EXPERTS, group, n_zl, width), (0, 2, 1, 3))
+        parts = parts.reshape(EXPERTS * n_zl, group, width)
+        outs = lax.all_to_all(parts, ("y", "zl"), split_axis=0, concat_axis=0, tiled=True)
         expert_cols = outs.reshape(EXPERTS * CAP, width).astype(jnp.float32)
         mixture = jnp.dot(combine[0], expert_cols, precision=lax.Precision.HIGHEST)
         layer_cols = (

time: 405 us -> 386 us (0.953)
  blocking collectives: 92.3 us -> 75.7 us
    all_to_all x3 -> x1, blocking collectives: 26.9 us -> 11.7 us  [per_device(): lax.all_to_all(rows, ('y', 'zl'), split_axis=0, concat_axis=0, tiled=True)]
    all_to_all x3 -> x2, starting transfers between devices: 15.3 us -> 13.5 us  [the longest x1 7.39 us: per_device(): lax.all_to_all(both_heads, CTX, split_axis=2, concat_axis=1, tiled=True)]
    unnamed x30 -> x28, local copies, waits for them, and re-layouts: 9.54 us -> 10.7 us
    all_to_all x3 -> x2, waiting for transfers between devices: 16.8 us -> 17.7 us  [the longest x1 11 us: per_device(): lax.all_to_all(both_heads, CTX, split_axis=2, concat_axis=1, tiled=True)]
  transfers between devices with their start and end apart: 9 -> 8, of which waited for: 8 -> 7; matrix products, arithmetic and copies ran while one was open for 3% -> 3% of each run, Pallas kernels for 0% -> 0%
where the time goes in v3:
time: 386 us
  waiting for transfers between devices  242 us (63%)
  blocking collectives  75.7 us (20%)
  matrix products  22.4 us (6%)
  local copies, waits for them, and re-layouts  15.6 us (4%)
  starting transfers between devices  14.6 us (4%)
  between operations  13.5 us (3%)
    all_gather x1, waiting for transfers between devices, per_device(): rows = lax.all_gather(rows, 'x', axis=0, tiled=True)  72.2 us
    reduce_scatter x1, waiting for transfers between devices, per_device(): parts = lax.psum_scatter(parts, 'x', scatter_dimension=0, tiled=True)  66.7 us
    psum x3, blocking collectives, row_scale(): lax.psum(jnp.sum(local_rows * local_rows, axis=-1, keepdims=True), CTX)  47.8 us
    reduce_scatter x1, waiting for transfers between devices, per_device(): lax.psum_scatter(parts, ('zh', 'zl'), scatter_dimension=0, tiled=False)  39 us
    all_gather x1, waiting for transfers between devices, per_device(): rows = lax.all_gather(rows, ('zh', 'zl'), axis=0, tiled=True)  36.2 us
    all_gather x1, blocking collectives, per_device(): layer_out = lax.all_gather(layer_cols, CTX, axis=1, tiled=True)  16.2 us
    all_to_all x1, blocking collectives, per_device(): lax.all_to_all(rows, ('y', 'zl'), split_axis=0, concat_axis=0, tiled=True)  11.7 us
    all_to_all x1, waiting for transfers between devices, per_device(): lax.all_to_all(both_heads, CTX, split_axis=2, concat_axis=1, tiled=True)  11 us
  transfers between devices with their start and end apart: 8, of which 7 were waited for; matrix products, arithmetic and copies ran while one was open for 3% of the time, Pallas kernels for 0%

profile of v3, /device:TPU:1, one launch (start us, length us, event | category | flops | bytes accessed | tf_op | source)
XLA Modules:
  0.0 385.6 jit_solution(8690284698438430779)
XLA Ops:
  6.5 1.1 copy.79
  9.9 7.4 %all-to-all-start = ((bf16[2,128,8,128]{3,1,0,2:T(8,128)(2,1)}), bf16[2,128,8,128]{3,1,0,2:T(8,128)(2,1)S(1)}, u32[]{:S(2)}, u32[]{:S(2)}) async-start(bf16[2,128,8,128]{3,1,0,2:T(8,128)(2,1)} %copy.80), calls=%async_computation | async-start | bytes 1048576 | tf_op jit(solution)/shard_map/attention/all_to_all | solution.py:101
  20.7 11.0 %all-to-all-done = bf16[2,128,8,128]{3,1,0,2:T(8,128)(2,1)S(1)} async-done(((bf16[2,128,8,128]{3,1,0,2:T(8,128)(2,1)}), bf16[2,128,8,128]{3,1,0,2:T(8,128)(2,1)S(1)}, u32[]{:S(2)}, u32[]{:S(2)}) %all-to-all-start) | async-done | bytes 524320 | tf_op jit(solution)/shard_map/attention/all_to_all | solution.py:101
  33.0 13.9 %psum.21 = f32[64,1]{0,1:T(1,128)S(1)} all-reduce(f32[64,1]{0,1:T(1,128)S(1)} %bitcast.178), channel_id=1, replica_groups=mesh['zl'=4,'core'=2,'y'=4,'x'=4,'zh'=2] {'zl','core'}, use_global_device_ids=true, to_apply=%region_3.4 | all-reduce | flops 64 | bytes 512 | tf_op jit(solution)/shard_map/norms/psum | solution.py:65
  48.4 14.6 %psum.22 = f32[64,1]{0,1:T(1,128)S(1)} all-reduce(f32[64,1]{0,1:T(1,128)S(1)} %bitcast.171), channel_id=1, replica_groups=mesh['zl'=4,'core'=2,'y'=4,'x'=4,'zh'=2] {'zl','core'}, use_global_device_ids=true, to_apply=%region_9.10 | all-reduce | flops 64 | bytes 512 | tf_op jit(solution)/shard_map/norms/psum | solution.py:65
  63.0 1.2 fusion.7
  64.2 11.7 %all_to_all.25 = bf16[16,8,768]{2,1,0:T(8,128)(2,1)} all-to-all(bf16[16,8,768]{2,1,0:T(8,128)(2,1)S(1)} %fusion.7), channel_id=1, replica_groups=mesh['zl'=4,'core'=2,'y'=4,'x'=4,'zh'=2] {'y','zl'}, dimensions={0} | all-to-all | bytes 393216 | tf_op jit(solution)/shard_map/dispatch/all_to_all | solution.py:135
  76.0 36.2 %all-gather.3.cloned.1.call-done = bf16[32,8,4,768]{3,1,2,0:T(8,128)(2,1)} async-done(((bf16[4,8,4,768]{3,1,2,0:T(8,128)(2,1)}), bf16[32,8,4,768]{3,1,2,0:T(8,128)(2,1)}) %all-gather.3.cloned.1.call-update) | async-done | bytes 1572880 | tf_op jit(solution)/shard_map/dispatch/all_gather | solution.py:137
  112.2 72.2 %all-gather.5.cloned.1.call-done = bf16[128,8,4,768]{3,1,2,0:T(8,128)(2,1)} async-done(((bf16[32,8,4,768]{3,1,2,0:T(8,128)(2,1)}), bf16[128,8,4,768]{3,1,2,0:T(8,128)(2,1)}) %all-gather.5.cloned.1.call-update) | async-done | bytes 6291472 | tf_op jit(solution)/shard_map/dispatch/all_gather | solution.py:138
  185.3 3.2 copy.88
  188.7 1.6 copy-done.2
  193.3 1.8 fusion.46
  195.1 1.8 fusion.47
  196.9 4.7 %fusion.16 = f32[1024,256]{1,0:T(8,128)S(1)} fusion(f32[1024,256]{1,0:T(8,128)S(1)} %fusion.46, bf16[1024,3072]{1,0:T(8,128)(2,1)} %collective-permute-done, bf16[3072,256]{1,0:T(8,128)(2,1)S(1)} %bitcast.162), kind=kOutput, calls=%fused_computation.27 | convolution fusion | flops 1612972032 | bytes 9961472 | tf_op jit(solution)/shard_map/experts/dot_general | solution.py:157
  201.7 4.6 %fusion.2 = bf16[1024,256]{1,0:T(8,128)(2,1)S(1)} fusion(f32[1024,256]{1,0:T(8,128)S(1)} %fusion.16, f32[1024,256]{1,0:T(8,128)S(1)} %fusion.47, bf16[1024,3072]{1,0:T(8,128)(2,1)} %collective-permute-done, bf16[3072,256]{1,0:T(8,128)(2,1)S(1)} %bitcast.161), kind=kOutput, calls=%fused_computation.9 | convolution fusion | flops 1611399168 | bytes 10485760 | tf_op jit(solution)/shard_map/experts/dot_general | solution.py:160
  206.3 1.8 convolution_convert_fusion
  208.2 10.1 %collective-permute-done.1 = bf16[1024,3072]{1,0:T(8,128)(2,1)S(1)} collective-permute-done((bf16[1024,3072]{1,0:T(8,128)(2,1)S(1)}, bf16[1024,3072]{1,0:T(8,128)(2,1)S(1)}, u32[]{:S(2)}, u32[]{:S(2)}) %collective-permute-start.1) | collective-permute-done | bytes 6291488 | tf_op jit(solution)/shard_map/combine/ppermute | solution.py:172
  218.4 4.5 %add_convert_fusion = bf16[1024,3072]{1,0:T(8,128)(2,1)} fusion(bf16[1024,3072]{1,0:T(8,128)(2,1)S(1)} %collective-permute-done.1, bf16[1024,256]{1,0:T(8,128)(2,1)S(1)} %fusion.2, bf16[256,3072]{0,1:T(8,128)(2,1)S(1)} %bitcast.152), kind=kOutput, calls=%fused_computation | convolution fusion | flops 1626341376 | bytes 14680064 | tf_op jit(solution)/shard_map/experts/dot_general | solution.py:164
  222.9 66.7 %reduce-scatter.3.cloned.1.call-done = bf16[32,8,4,768]{3,1,2,0:T(8,128)(2,1)} async-done(((bf16[128,8,4,768]{3,1,2,0:T(8,128)(2,1)}), bf16[32,8,4,768]{3,1,2,0:T(8,128)(2,1)}) %reduce-scatter.3.cloned.1.call-update) | async-done | bytes 1572880 | tf_op jit(solution)/shard_map/combine/reduce_scatter | solution.py:175
  289.7 39.0 %reduce-scatter.5.cloned.1.call-done = bf16[1,4,8,4,768]{4,2,3,1,0:T(8,128)(2,1)} async-done(((bf16[8,4,8,4,768]{4,2,3,1,0:T(8,128)(2,1)}), bf16[1,4,8,4,768]{4,2,3,1,0:T(8,128)(2,1)}) %reduce-scatter.5.cloned.1.call-update) | async-done | bytes 196624 | tf_op jit(solution)/shard_map/combine/reduce_scatter | solution.py:177
  328.6 6.1 %all-to-all-start.2 = ((bf16[16,8,768]{2,1,0:T(8,128)(2,1)}), bf16[16,8,768]{2,1,0:T(8,128)(2,1)S(1)}, u32[]{:S(2)}, u32[]{:S(2)}) async-start(bf16[16,8,768]{2,1,0:T(8,128)(2,1)} %bitcast.170), calls=%async_computation.4 | async-start | bytes 393216 | tf_op jit(solution)/shard_map/combine/all_to_all | solution.py:180
  335.6 6.7 %all-to-all-done.2 = bf16[16,8,768]{2,1,0:T(8,128)(2,1)S(1)} async-done(((bf16[16,8,768]{2,1,0:T(8,128)(2,1)}), bf16[16,8,768]{2,1,0:T(8,128)(2,1)S(1)}, u32[]{:S(2)}, u32[]{:S(2)}) %all-to-all-start.2) | async-done | bytes 196640 | tf_op jit(solution)/shard_map/combine/all_to_all | solution.py:180
  342.6 19.3 %psum.23 = f32[64,1]{0,1:T(1,128)S(1)} all-reduce(f32[64,1]{0,1:T(1,128)S(1)} %bitcast.172), channel_id=1, replica_groups=mesh['zl'=4,'core'=2,'y'=4,'x'=4,'zh'=2] {'zl','core'}, use_global_device_ids=true, to_apply=%region_13.14 | all-reduce | flops 64 | bytes 512 | tf_op jit(solution)/shard_map/combine/psum | solution.py:65
  362.1 16.2 %all_gather.11 = bf16[64,6144]{1,0:T(8,128)(2,1)S(1)} all-gather(bf16[64,768]{1,0:T(8,128)(2,1)S(1)} %fusion.19), channel_id=1, replica_groups=mesh['zl'=4,'core'=2,'y'=4,'x'=4,'zh'=2] {'zl','core'}, dimensions={1}, use_global_device_ids=true | all-gather | bytes 884736 | tf_op jit(solution)/shard_map/combine/all_gather | solution.py:186
  (73 shorter events, 14.7 us)
Async XLA Ops:
  6.5 13.9 %copy-start = (bf16[1,64,128]{2,1,0:T(8,128)(2,1)S(1)}, bf16[1,64,128]{2,1,0:T(8,128)(2,1)}, u32[]{:S(2)}) copy-start(bf16[1,64,128]{2,1,0:T(8,128)(2,1)} %param.19) | copy-start | bytes 49156
  8.8 8.5 %copy-start.8 = (s32[1,64]{1,0:T(1,128)S(1)}, s32[1,64]{1,0:T(1,128)}, u32[]{:S(2)}) copy-start(s32[1,64]{1,0:T(1,128)} %param.20) | copy-start | bytes 772
  8.8 8.5 %copy-start.5 = (s32[1,64,2]{1,2,0:T(2,128)S(1)}, s32[1,64,2]{1,2,0:T(2,128)}, u32[]{:S(2)}) copy-start(s32[1,64,2]{1,2,0:T(2,128)} %param.22) | copy-start | bytes 1540
  8.8 9.4 %copy-start.6 = (s32[1,64,2]{1,2,0:T(2,128)S(1)}, s32[1,64,2]{1,2,0:T(2,128)}, u32[]{:S(2)}) copy-start(s32[1,64,2]{1,2,0:T(2,128)} %param.23) | copy-start | bytes 1540
  8.8 9.6 %copy-start.4 = (bf16[1,64,768]{2,1,0:T(8,128)(2,1)S(1)}, bf16[1,64,768]{2,1,0:T(8,128)(2,1)}, u32[]{:S(2)}) copy-start(bf16[1,64,768]{2,1,0:T(8,128)(2,1)} %param.15) | copy-start | bytes 294916
  8.9 11.3 %copy-start.7 = (bf16[1,64,128]{2,1,0:T(8,128)(2,1)S(1)}, bf16[1,64,128]{2,1,0:T(8,128)(2,1)}, u32[]{:S(2)}) copy-start(bf16[1,64,128]{2,1,0:T(8,128)(2,1)} %param.18) | copy-start | bytes 49156
  9.9 21.8 %all-to-all-start = ((bf16[2,128,8,128]{3,1,0,2:T(8,128)(2,1)}), bf16[2,128,8,128]{3,1,0,2:T(8,128)(2,1)S(1)}, u32[]{:S(2)}, u32[]{:S(2)}) async-start(bf16[2,128,8,128]{3,1,0,2:T(8,128)(2,1)} %copy.80), calls=%async_computation | async-start | bytes 1048576 | tf_op jit(solution)/shard_map/attention/all_to_all | solution.py:101
  17.3 94.8 %all-gather.3.cloned.1.call-start = ((), (), s32[]{:S(2)}) async-start(), calls=%async_computation.5 | async-start | bytes 1769472 | tf_op jit(solution)/shard_map/dispatch/all_gather | solution.py:137
  76.0 108.5 %all-gather.5.cloned.1.call-start = ((), (), s32[]{:S(2)}) async-start(), calls=%async_computation.6 | async-start | bytes 7864320 | tf_op jit(solution)/shard_map/dispatch/all_gather | solution.py:138
  112.2 177.4 %reduce-scatter.3.cloned.1.call-start = ((), (), s32[]{:S(2)}) async-start(), calls=%async_computation.7 | async-start | bytes 7864320 | tf_op jit(solution)/shard_map/combine/reduce_scatter | solution.py:175
  184.4 12.5 %collective-permute-start = (bf16[1024,3072]{1,0:T(8,128)(2,1)}, bf16[1024,3072]{1,0:T(8,128)(2,1)}, u32[]{:S(2)}, u32[]{:S(2)}) collective-permute-start(bf16[1024,3072]{1,0:T(8,128)(2,1)} %bitcast.173), channel_id=1, source_target_pairs={{0,32},{32,0},{1,33},{33,1},{2,34},{34,2},{3,35},{35,3},{4,36},{36... | collective-permute-start | bytes 18874376 | tf_op jit(solution)/shard_map/dispatch/ppermute | solution.py:140
  188.5 1.9 copy-start.2
  188.5 2.8 copy-start.3
  188.5 4.0 %slice-start = ((s8[6291456]{0:T(1024)(128)(4,1)}), s8[4194304]{0:T(1024)(128)(4,1)S(1)}, s32[]{:S(2)}) async-start(s8[6291456]{0:T(1024)(128)(4,1)} %bitcast.174), calls=%async_computation.9 | async-start | bytes 8388608
  191.3 2.0 slice-start.1
  208.1 10.2 %collective-permute-start.1 = (bf16[1024,3072]{1,0:T(8,128)(2,1)S(1)}, bf16[1024,3072]{1,0:T(8,128)(2,1)S(1)}, u32[]{:S(2)}, u32[]{:S(2)}) collective-permute-start(bf16[1024,3072]{1,0:T(8,128)(2,1)S(1)} %convolution_convert_fusion), channel_id=1, source_target_pairs={{0,32},{32,0},{1,33},{33,1},{2,34},{34,2},{3,35},{35,3},{4,36},{36... | collective-permute-start | bytes 18874376 | tf_op jit(solution)/shard_map/combine/ppermute | solution.py:172
  222.9 105.8 %reduce-scatter.5.cloned.1.call-start = ((), (), s32[]{:S(2)}) async-start(), calls=%async_computation.8 | async-start | bytes 1769472 | tf_op jit(solution)/shard_map/combine/reduce_scatter | solution.py:177
  328.6 13.7 %all-to-all-start.2 = ((bf16[16,8,768]{2,1,0:T(8,128)(2,1)}), bf16[16,8,768]{2,1,0:T(8,128)(2,1)S(1)}, u32[]{:S(2)}, u32[]{:S(2)}) async-start(bf16[16,8,768]{2,1,0:T(8,128)(2,1)} %bitcast.170), calls=%async_computation.4 | async-start | bytes 393216 | tf_op jit(solution)/shard_map/combine/all_to_all | solution.py:180
  342.3 36.8 %copy-start.1 = (bf16[1,64,128]{2,1,0:T(8,128)(2,1)S(1)}, bf16[1,64,128]{2,1,0:T(8,128)(2,1)}, u32[]{:S(2)}) copy-start(bf16[1,64,128]{2,1,0:T(8,128)(2,1)} %param.19) | copy-start | bytes 49156
Sparse Core Ops, SparseCore 0:
  76.1 36.0 all-gather.2
  114.0 70.4 all-gather.4
  223.0 66.5 reduce-scatter.2
  292.0 36.5 reduce-scatter.4

commit v4 on v3

--- a/solution.py
+++ b/solution.py
@@ -135,9 +135,17 @@
         rows = lax.all_to_all(rows, ("y", "zl"), split_axis=0, concat_axis=0, tiled=True)
         rows = jnp.transpose(rows.reshape(EXPERTS, n_zl, group, width), (0, 2, 1, 3))
         rows = lax.all_gather(rows, ("zh", "zl"), axis=0, tiled=True)
-        rows = lax.all_gather(rows, "x", axis=0, tiled=True)
-        own_rows = rows.reshape(-1, n_zl * width)
-        other_rows = lax.ppermute(own_rows, "core", swap)
+        block = rows.reshape(-1, n_zl * width)
+        half = block.shape[0] // 2
+        n_x = lax.axis_size("x")
+        fwd = [(i, (i + 1) % n_x) for i in range(n_x)]
+        bwd = [(i, (i - 1) % n_x) for i in range(n_x)]
+        from_prev = lax.ppermute(block, "x", fwd)
+        from_next = lax.ppermute(block, "x", bwd)
+        far = jnp.concatenate(
+            [lax.ppermute(from_prev[:half], "x", fwd), lax.ppermute(from_next[half:], "x", bwd)]
+        )
+        own_blocks = [block, from_next, far, from_prev]
 
     with jax.named_scope("experts"):
         core = lax.axis_index("core")
@@ -154,25 +162,43 @@
         gate_own, gate_other = halves(w_gate[0], 0)
         up_own, up_other = halves(w_up[0], 0)
         down_own, down_other = halves(w_down[0], 1)
-        pre_gate = jnp.dot(own_rows, gate_own, preferred_element_type=jnp.float32) + jnp.dot(
-            other_rows, gate_other, preferred_element_type=jnp.float32
-        )
-        pre_up = jnp.dot(own_rows, up_own, preferred_element_type=jnp.float32) + jnp.dot(
-            other_rows, up_other, preferred_element_type=jnp.float32
-        )
-        hidden_units = (jax.nn.gelu(pre_gate) * pre_up).astype(jnp.bfloat16)
-        piece_own = jnp.dot(hidden_units, down_own, preferred_element_type=jnp.float32).astype(
-            jnp.bfloat16
-        )
-        piece_other = jnp.dot(
-            hidden_units, down_other, preferred_element_type=jnp.float32
+
+        def expert_block(own_rows):
+            other_rows = lax.ppermute(own_rows, "core", swap)
+            pre_gate = jnp.dot(own_rows, gate_own, preferred_element_type=jnp.float32) + jnp.dot(
+                other_rows, gate_other, preferred_element_type=jnp.float32
+            )
+            pre_up = jnp.dot(own_rows, up_own, preferred_element_type=jnp.float32) + jnp.dot(
+                other_rows, up_other, preferred_element_type=jnp.float32
+            )
+            hidden_units = (jax.nn.gelu(pre_gate) * pre_up).astype(jnp.bfloat16)
+            piece_own = jnp.dot(
+                hidden_units, down_own, preferred_element_type=jnp.float32
+            ).astype(jnp.bfloat16)
+            piece_other = jnp.dot(
+                hidden_units, down_other, preferred_element_type=jnp.float32
+            ).astype(jnp.bfloat16)
+            received = lax.ppermute(piece_other, "core", swap)
+            return piece_own.astype(jnp.float32) + received.astype(jnp.float32)
+
+        sums = [expert_block(b) for b in own_blocks]
+
+    with jax.named_scope("combine"):
+        to_next = lax.ppermute(sums[2][:half].astype(jnp.bfloat16), "x", fwd)
+        to_prev = lax.ppermute(sums[2][half:].astype(jnp.bfloat16), "x", bwd)
+        pad = jnp.zeros_like(to_next)
+        send_next = (sums[1] + jnp.concatenate([to_next, pad]).astype(jnp.float32)).astype(
+            jnp.bfloat16
+        )
+        send_prev = (sums[3] + jnp.concatenate([pad, to_prev]).astype(jnp.float32)).astype(
+            jnp.bfloat16
+        )
+        got_prev = lax.ppermute(send_next, "x", fwd)
+        got_next = lax.ppermute(send_prev, "x", bwd)
+        parts = (
+            sums[0] + got_prev.astype(jnp.float32) + got_next.astype(jnp.float32)
         ).astype(jnp.bfloat16)
-
-    with jax.named_scope("combine"):
-        received = lax.ppermute(piece_other, "core", swap)
-        parts = (piece_own.astype(jnp.float32) + received.astype(jnp.float32)).astype(jnp.bfloat16)
         parts = parts.reshape(rows.shape)
-        parts = lax.psum_scatter(parts, "x", scatter_dimension=0, tiled=True)
         parts = parts.reshape((2 * n_zl, -1) + parts.shape[1:])
         parts = lax.psum_scatter(parts, ("zh", "zl"), scatter_dimension=0, tiled=False)
         parts = jnp.transpose(parts.reshape(EXPERTS, group, n_zl, width), (0, 2, 1, 3))

time: 386 us -> 343 us (0.89)
  waiting for transfers between devices: 242 us -> 166 us
  starting transfers between devices: 14.6 us -> 40.8 us
  local copies, waits for them, and re-layouts: 15.6 us -> 20.4 us
    all_gather x1 -> x0, waiting for transfers between devices: 72.2 us -> none  [per_device(): rows = lax.all_gather(rows, 'x', axis=0, tiled=True)]
    ppermute x2 -> x16, waiting for transfers between devices: 10.1 us -> 78.5 us  [the longest x1 31 us: per_device(): got_next = lax.ppermute(send_prev, 'x', bwd)]
    reduce_scatter x1 -> x0, waiting for transfers between devices: 66.7 us -> none  [per_device(): parts = lax.psum_scatter(parts, 'x', scatter_dimension=0, tiled=True)]
    ppermute x2 -> x16, starting transfers between devices: 0.93 us -> 27.3 us  [the longest x4 12.9 us: expert_block(): other_rows = lax.ppermute(own_rows, 'core', swap)]
    reduce_scatter x1, waiting for transfers between devices: 39 us -> 33.9 us  [per_device(): lax.psum_scatter(parts, ('zh', 'zl'), scatter_dimension=0, tiled=False)]
    unnamed x28 -> x31, local copies, waits for them, and re-layouts: 10.7 us -> 13.1 us
    dot_general x6 -> x24, matrix products: 19.2 us -> 17.3 us  [the longest x4 3.78 us: expert_block(): jnp.dot(own_rows, gate_own, preferred_element_type=jnp.float32)]
  transfers between devices with their start and end apart: 8 -> 20, of which waited for: 7 -> 8; matrix products, arithmetic and copies ran while one was open for 3% -> 8% of each run, Pallas kernels for 0% -> 0%
where the time goes in v4:
time: 343 us; the launch traced here: 342 us
  waiting for transfers between devices  166 us (48%)
  blocking collectives  75.7 us (22%)
  starting transfers between devices  40.8 us (12%)
  local copies, waits for them, and re-layouts  20.4 us (6%)
  matrix products  20.4 us (6%)
  between operations  14 us (4%)
  other arithmetic  4.08 us (1%)
    psum x3, blocking collectives, row_scale(): lax.psum(jnp.sum(local_rows * local_rows, axis=-1, keepdims=True), CTX)  47.9 us
    all_gather x1, waiting for transfers between devices, per_device(): rows = lax.all_gather(rows, ('zh', 'zl'), axis=0, tiled=True)  36.2 us
    reduce_scatter x1, waiting for transfers between devices, per_device(): lax.psum_scatter(parts, ('zh', 'zl'), scatter_dimension=0, tiled=False)  33.9 us
    ppermute x1, waiting for transfers between devices, per_device(): got_next = lax.ppermute(send_prev, 'x', bwd)  31 us
    ppermute x1, waiting for transfers between devices, per_device(): from_prev = lax.ppermute(block, 'x', fwd)  30.2 us
    all_gather x1, blocking collectives, per_device(): layer_out = lax.all_gather(layer_cols, CTX, axis=1, tiled=True)  16.2 us
    ppermute x1, waiting for transfers between devices, per_device(): to_prev = lax.ppermute(sums[2][half:].astype(jnp.bfloat16), 'x', bwd)  13.4 us
    unnamed x31, local copies, waits for them, and re-layouts  13.1 us
  transfers between devices with their start and end apart: 20, of which 8 were waited for; matrix products, arithmetic and copies ran while one was open for 8% of the time, Pallas kernels for 0%

profile of v4, /device:TPU:1, one launch (start us, length us, event | category | flops | bytes accessed | tf_op | source)
XLA Modules:
  0.0 341.8 jit_solution(17508466482970802142)
XLA Ops:
  9.9 7.4 %all-to-all-start = ((bf16[2,128,8,128]{3,1,0,2:T(8,128)(2,1)}), bf16[2,128,8,128]{3,1,0,2:T(8,128)(2,1)S(1)}, u32[]{:S(2)}, u32[]{:S(2)}) async-start(bf16[2,128,8,128]{3,1,0,2:T(8,128)(2,1)} %copy.80), calls=%async_computation | async-start | bytes 1048576 | tf_op jit(solution)/shard_map/attention/all_to_all | solution.py:101
  20.7 11.0 %all-to-all-done = bf16[2,128,8,128]{3,1,0,2:T(8,128)(2,1)S(1)} async-done(((bf16[2,128,8,128]{3,1,0,2:T(8,128)(2,1)}), bf16[2,128,8,128]{3,1,0,2:T(8,128)(2,1)S(1)}, u32[]{:S(2)}, u32[]{:S(2)}) %all-to-all-start) | async-done | bytes 524320 | tf_op jit(solution)/shard_map/attention/all_to_all | solution.py:101
  33.0 13.9 %psum.21 = f32[64,1]{0,1:T(1,128)S(1)} all-reduce(f32[64,1]{0,1:T(1,128)S(1)} %bitcast.230), channel_id=1, replica_groups=mesh['zl'=4,'core'=2,'y'=4,'x'=4,'zh'=2] {'zl','core'}, use_global_device_ids=true, to_apply=%region_3.4 | all-reduce | flops 64 | bytes 512 | tf_op jit(solution)/shard_map/norms/psum | solution.py:65
  48.4 14.6 %psum.22 = f32[64,1]{0,1:T(1,128)S(1)} all-reduce(f32[64,1]{0,1:T(1,128)S(1)} %bitcast.228), channel_id=1, replica_groups=mesh['zl'=4,'core'=2,'y'=4,'x'=4,'zh'=2] {'zl','core'}, use_global_device_ids=true, to_apply=%region_9.10 | all-reduce | flops 64 | bytes 512 | tf_op jit(solution)/shard_map/norms/psum | solution.py:65
  64.2 11.7 %all_to_all.25 = bf16[16,8,768]{2,1,0:T(8,128)(2,1)} all-to-all(bf16[16,8,768]{2,1,0:T(8,128)(2,1)S(1)} %fusion.15), channel_id=1, replica_groups=mesh['zl'=4,'core'=2,'y'=4,'x'=4,'zh'=2] {'y','zl'}, dimensions={0} | all-to-all | bytes 393216 | tf_op jit(solution)/shard_map/dispatch/all_to_all | solution.py:135
  76.0 36.2 %all-gather.2.cloned.1.call-done = bf16[32,8,4,768]{3,1,2,0:T(8,128)(2,1)} async-done(((bf16[4,8,4,768]{3,1,2,0:T(8,128)(2,1)}), bf16[32,8,4,768]{3,1,2,0:T(8,128)(2,1)}) %all-gather.2.cloned.1.call-update) | async-done | bytes 1572880 | tf_op jit(solution)/shard_map/dispatch/all_gather | solution.py:137
  114.8 30.2 %collective-permute-done.5 = bf16[256,3072]{1,0:T(8,128)(2,1)S(1)} collective-permute-done((bf16[256,3072]{1,0:T(8,128)(2,1)}, bf16[256,3072]{1,0:T(8,128)(2,1)S(1)}, u32[]{:S(2)}, u32[]{:S(2)}) %collective-permute-start.5) | collective-permute-done | bytes 1572896 | tf_op jit(solution)/shard_map/dispatch/ppermute | solution.py:143
  147.2 3.2 copy.88
  151.6 2.7 collective-permute-start.7
  158.5 5.9 %collective-permute-start = (bf16[256,3072]{1,0:T(8,128)(2,1)S(1)}, bf16[256,3072]{1,0:T(8,128)(2,1)S(1)}, u32[]{:S(2)}, u32[]{:S(2)}) collective-permute-start(bf16[256,3072]{1,0:T(8,128)(2,1)S(1)} %bitcast.213), channel_id=1, source_target_pairs={{0,32},{32,0},{1,33},{33,1},{2,34},{34,2},{3,35},{35,3},{4,36},{36... | collective-permute-start | bytes 4718600 | tf_op jit(solution)/shard_map/experts/ppermute | solution.py:167
  165.7 6.5 %collective-permute-start.8 = (bf16[256,3072]{1,0:T(8,128)(2,1)S(1)}, bf16[256,3072]{1,0:T(8,128)(2,1)S(1)}, u32[]{:S(2)}, u32[]{:S(2)}) collective-permute-start(bf16[256,3072]{1,0:T(8,128)(2,1)S(1)} %constant_dynamic-update-slice_fusion), channel_id=1, source_target_pairs={{0,32},{32,0},{1,33},{33,1},{2,34},{34,2},{3,35},{35,3},{4,36},{36... | collective-permute-start | bytes 4718600 | tf_op jit(solution)/shard_map/experts/ppermute | solution.py:167
  175.8 2.0 fusion.80
  177.8 2.0 fusion.81
  188.1 3.5 %collective-permute-start.14 = (bf16[128,3072]{1,0:T(8,128)(2,1)S(1)}, bf16[128,3072]{1,0:T(8,128)(2,1)S(1)}, u32[]{:S(2)}, u32[]{:S(2)}) collective-permute-start(bf16[128,3072]{1,0:T(8,128)(2,1)S(1)} %get-tuple-element.16), channel_id=1, source_target_pairs={{0,6},{2,0},{4,2},{6,4},{1,7},{3,1},{5,3},{7,5},{8,14},{10,8},{12,... | collective-permute-start | bytes 2359304 | tf_op jit(solution)/shard_map/combine/ppermute | solution.py:188
  194.6 13.4 %collective-permute-done.14 = bf16[128,3072]{1,0:T(8,128)(2,1)S(1)} collective-permute-done((bf16[128,3072]{1,0:T(8,128)(2,1)S(1)}, bf16[128,3072]{1,0:T(8,128)(2,1)S(1)}, u32[]{:S(2)}, u32[]{:S(2)}) %collective-permute-start.14) | collective-permute-done | bytes 786464 | tf_op jit(solution)/shard_map/combine/ppermute | solution.py:188
  208.7 3.5 %collective-permute-start.15 = (bf16[256,3072]{1,0:T(8,128)(2,1)S(1)}, bf16[256,3072]{1,0:T(8,128)(2,1)S(1)}, u32[]{:S(2)}, u32[]{:S(2)}) collective-permute-start(bf16[256,3072]{1,0:T(8,128)(2,1)S(1)} %add_convert_fusion.1), channel_id=1, source_target_pairs={{0,6},{2,0},{4,2},{6,4},{1,7},{3,1},{5,3},{7,5},{8,14},{10,8},{12,... | collective-permute-start | bytes 4718600 | tf_op jit(solution)/shard_map/combine/ppermute | solution.py:197
  213.5 31.0 %collective-permute-done.15 = bf16[256,3072]{1,0:T(8,128)(2,1)S(1)} collective-permute-done((bf16[256,3072]{1,0:T(8,128)(2,1)S(1)}, bf16[256,3072]{1,0:T(8,128)(2,1)S(1)}, u32[]{:S(2)}, u32[]{:S(2)}) %collective-permute-start.15) | collective-permute-done | bytes 1572896 | tf_op jit(solution)/shard_map/combine/ppermute | solution.py:197
  244.6 3.9 %collective-permute-done.11 = bf16[256,3072]{1,0:T(8,128)(2,1)S(1)} collective-permute-done((bf16[256,3072]{1,0:T(8,128)(2,1)S(1)}, bf16[256,3072]{1,0:T(8,128)(2,1)S(1)}, u32[]{:S(2)}, u32[]{:S(2)}) %collective-permute-start.11) | collective-permute-done | bytes 1572896 | tf_op jit(solution)/shard_map/combine/ppermute | solution.py:196
  248.4 2.1 add_convert_fusion
  250.6 33.9 %reduce-scatter.2.cloned.1.call-done = bf16[1,4,8,4,768]{4,2,3,1,0:T(8,128)(2,1)} async-done(((bf16[8,4,8,4,768]{4,2,3,1,0:T(8,128)(2,1)}), bf16[1,4,8,4,768]{4,2,3,1,0:T(8,128)(2,1)}) %reduce-scatter.2.cloned.1.call-update) | async-done | bytes 196624 | tf_op jit(solution)/shard_map/combine/reduce_scatter | solution.py:203
  284.5 6.1 %all-to-all-start.2 = ((bf16[16,8,768]{2,1,0:T(8,128)(2,1)}), bf16[16,8,768]{2,1,0:T(8,128)(2,1)S(1)}, u32[]{:S(2)}, u32[]{:S(2)}) async-start(bf16[16,8,768]{2,1,0:T(8,128)(2,1)} %bitcast.227), calls=%async_computation.3 | async-start | bytes 393216 | tf_op jit(solution)/shard_map/combine/all_to_all | solution.py:206
  291.4 6.7 %all-to-all-done.2 = bf16[16,8,768]{2,1,0:T(8,128)(2,1)S(1)} async-done(((bf16[16,8,768]{2,1,0:T(8,128)(2,1)}), bf16[16,8,768]{2,1,0:T(8,128)(2,1)S(1)}, u32[]{:S(2)}, u32[]{:S(2)}) %all-to-all-start.2) | async-done | bytes 196640 | tf_op jit(solution)/shard_map/combine/all_to_all | solution.py:206
  298.5 19.3 %psum.23 = f32[64,1]{0,1:T(1,128)S(1)} all-reduce(f32[64,1]{0,1:T(1,128)S(1)} %bitcast.229), channel_id=1, replica_groups=mesh['zl'=4,'core'=2,'y'=4,'x'=4,'zh'=2] {'zl','core'}, use_global_device_ids=true, to_apply=%region_12.13 | all-reduce | flops 64 | bytes 512 | tf_op jit(solution)/shard_map/combine/psum | solution.py:65
  317.9 16.2 %all_gather.7 = bf16[64,6144]{1,0:T(8,128)(2,1)S(1)} all-gather(bf16[64,768]{1,0:T(8,128)(2,1)S(1)} %fusion.50), channel_id=1, replica_groups=mesh['zl'=4,'core'=2,'y'=4,'x'=4,'zh'=2] {'zl','core'}, dimensions={1}, use_global_device_ids=true | all-gather | bytes 884736 | tf_op jit(solution)/shard_map/combine/all_gather | solution.py:212
  (120 shorter events, 41.0 us)
Async XLA Ops:
  6.5 13.9 %copy-start = (bf16[1,64,128]{2,1,0:T(8,128)(2,1)S(1)}, bf16[1,64,128]{2,1,0:T(8,128)(2,1)}, u32[]{:S(2)}) copy-start(bf16[1,64,128]{2,1,0:T(8,128)(2,1)} %param.19) | copy-start | bytes 49156
  8.8 9.6 %copy-start.7 = (bf16[1,64,768]{2,1,0:T(8,128)(2,1)S(1)}, bf16[1,64,768]{2,1,0:T(8,128)(2,1)}, u32[]{:S(2)}) copy-start(bf16[1,64,768]{2,1,0:T(8,128)(2,1)} %param.15) | copy-start | bytes 294916
  8.9 11.3 %copy-start.10 = (bf16[1,64,128]{2,1,0:T(8,128)(2,1)S(1)}, bf16[1,64,128]{2,1,0:T(8,128)(2,1)}, u32[]{:S(2)}) copy-start(bf16[1,64,128]{2,1,0:T(8,128)(2,1)} %param.18) | copy-start | bytes 49156
  9.9 21.8 %all-to-all-start = ((bf16[2,128,8,128]{3,1,0,2:T(8,128)(2,1)}), bf16[2,128,8,128]{3,1,0,2:T(8,128)(2,1)S(1)}, u32[]{:S(2)}, u32[]{:S(2)}) async-start(bf16[2,128,8,128]{3,1,0,2:T(8,128)(2,1)} %copy.80), calls=%async_computation | async-start | bytes 1048576 | tf_op jit(solution)/shard_map/attention/all_to_all | solution.py:101
  17.3 94.8 %all-gather.2.cloned.1.call-start = ((), (), s32[]{:S(2)}) async-start(), calls=%async_computation.4 | async-start | bytes 1769472 | tf_op jit(solution)/shard_map/dispatch/all_gather | solution.py:137
  75.9 208.6 %reduce-scatter.2.cloned.1.call-start = ((), (), s32[]{:S(2)}) async-start(), calls=%async_computation.5 | async-start | bytes 1769472 | tf_op jit(solution)/shard_map/combine/reduce_scatter | solution.py:203
  112.2 32.9 %collective-permute-start.5 = (bf16[256,3072]{1,0:T(8,128)(2,1)}, bf16[256,3072]{1,0:T(8,128)(2,1)S(1)}, u32[]{:S(2)}, u32[]{:S(2)}) collective-permute-start(bf16[256,3072]{1,0:T(8,128)(2,1)} %bitcast.211), channel_id=1, source_target_pairs={{0,2},{2,4},{4,6},{6,0},{1,3},{3,5},{5,7},{7,1},{8,10},{10,12},{12... | collective-permute-start | bytes 4718600 | tf_op jit(solution)/shard_map/dispatch/ppermute | solution.py:143
  113.4 37.0 %collective-permute-start.2 = (bf16[256,3072]{1,0:T(8,128)(2,1)}, bf16[256,3072]{1,0:T(8,128)(2,1)}, u32[]{:S(2)}, u32[]{:S(2)}) collective-permute-start(bf16[256,3072]{1,0:T(8,128)(2,1)} %bitcast.212), channel_id=1, source_target_pairs={{0,6},{2,0},{4,2},{6,4},{1,7},{3,1},{5,3},{7,5},{8,14},{10,8},{12,... | collective-permute-start | bytes 4718600 | tf_op jit(solution)/shard_map/dispatch/ppermute | solution.py:144
  147.1 17.3 %collective-permute-start.6 = (bf16[128,3072]{1,0:T(8,128)(2,1)}, bf16[128,3072]{1,0:T(8,128)(2,1)}, u32[]{:S(2)}, u32[]{:S(2)}) collective-permute-start(bf16[128,3072]{1,0:T(8,128)(2,1)} %slice.30), channel_id=1, source_target_pairs={{0,2},{2,4},{4,6},{6,0},{1,3},{3,5},{5,7},{7,1},{8,10},{10,12},{12... | collective-permute-start | bytes 2359304 | tf_op jit(solution)/shard_map/dispatch/ppermute | solution.py:146
  151.6 14.0 %collective-permute-start.7 = (bf16[128,3072]{1,0:T(8,128)(2,1)S(1)}, bf16[128,3072]{1,0:T(8,128)(2,1)S(1)}, u32[]{:S(2)}, u32[]{:S(2)}) collective-permute-start(bf16[128,3072]{1,0:T(8,128)(2,1)S(1)} %slice.31), channel_id=1, source_target_pairs={{0,6},{2,0},{4,2},{6,4},{1,7},{3,1},{5,3},{7,5},{8,14},{10,8},{12,... | collective-permute-start | bytes 2359304 | tf_op jit(solution)/shard_map/dispatch/ppermute | solution.py:146
  158.5 33.1 %collective-permute-start = (bf16[256,3072]{1,0:T(8,128)(2,1)S(1)}, bf16[256,3072]{1,0:T(8,128)(2,1)S(1)}, u32[]{:S(2)}, u32[]{:S(2)}) collective-permute-start(bf16[256,3072]{1,0:T(8,128)(2,1)S(1)} %bitcast.213), channel_id=1, source_target_pairs={{0,32},{32,0},{1,33},{33,1},{2,34},{34,2},{3,35},{35,3},{4,36},{36... | collective-permute-start | bytes 4718600 | tf_op jit(solution)/shard_map/experts/ppermute | solution.py:167
  165.7 14.1 %collective-permute-start.8 = (bf16[256,3072]{1,0:T(8,128)(2,1)S(1)}, bf16[256,3072]{1,0:T(8,128)(2,1)S(1)}, u32[]{:S(2)}, u32[]{:S(2)}) collective-permute-start(bf16[256,3072]{1,0:T(8,128)(2,1)S(1)} %constant_dynamic-update-slice_fusion), channel_id=1, source_target_pairs={{0,32},{32,0},{1,33},{33,1},{2,34},{34,2},{3,35},{35,3},{4,36},{36... | collective-permute-start | bytes 4718600 | tf_op jit(solution)/shard_map/experts/ppermute | solution.py:167
  174.2 8.9 %collective-permute-start.12 = (bf16[256,3072]{1,0:T(8,128)(2,1)S(1)}, bf16[256,3072]{1,0:T(8,128)(2,1)S(1)}, u32[]{:S(2)}, u32[]{:S(2)}) collective-permute-start(bf16[256,3072]{1,0:T(8,128)(2,1)S(1)} %copy-done.3), channel_id=1, source_target_pairs={{0,32},{32,0},{1,33},{33,1},{2,34},{34,2},{3,35},{35,3},{4,36},{36... | collective-permute-start | bytes 4718600 | tf_op jit(solution)/shard_map/experts/ppermute | solution.py:167
  174.2 11.3 %collective-permute-start.3 = (bf16[256,3072]{1,0:T(8,128)(2,1)}, bf16[256,3072]{1,0:T(8,128)(2,1)S(1)}, u32[]{:S(2)}, u32[]{:S(2)}) collective-permute-start(bf16[256,3072]{1,0:T(8,128)(2,1)} %collective-permute-done.2), channel_id=1, source_target_pairs={{0,32},{32,0},{1,33},{33,1},{2,34},{34,2},{3,35},{35,3},{4,36},{36... | collective-permute-start | bytes 4718600 | tf_op jit(solution)/shard_map/experts/ppermute | solution.py:167
  182.9 4.5 %collective-permute-start.9 = (bf16[256,3072]{1,0:T(8,128)(2,1)S(1)}, bf16[256,3072]{1,0:T(8,128)(2,1)S(1)}, u32[]{:S(2)}, u32[]{:S(2)}) collective-permute-start(bf16[256,3072]{1,0:T(8,128)(2,1)S(1)} %convolution_convert_fusion.2), channel_id=1, source_target_pairs={{0,32},{32,0},{1,33},{33,1},{2,34},{34,2},{3,35},{35,3},{4,36},{36... | collective-permute-start | bytes 4718600 | tf_op jit(solution)/shard_map/experts/ppermute | solution.py:181
  184.8 9.8 %collective-permute-start.13 = (bf16[256,3072]{1,0:T(8,128)(2,1)S(1)}, bf16[256,3072]{1,0:T(8,128)(2,1)S(1)}, u32[]{:S(2)}, u32[]{:S(2)}) collective-permute-start(bf16[256,3072]{1,0:T(8,128)(2,1)S(1)} %convolution_convert_fusion), channel_id=1, source_target_pairs={{0,32},{32,0},{1,33},{33,1},{2,34},{34,2},{3,35},{35,3},{4,36},{36... | collective-permute-start | bytes 4718600 | tf_op jit(solution)/shard_map/experts/ppermute | solution.py:181
  187.3 24.9 %collective-permute-start.4 = (bf16[256,3072]{1,0:T(8,128)(2,1)S(1)}, bf16[256,3072]{1,0:T(8,128)(2,1)S(1)}, u32[]{:S(2)}, u32[]{:S(2)}) collective-permute-start(bf16[256,3072]{1,0:T(8,128)(2,1)S(1)} %convolution_convert_fusion.4), channel_id=1, source_target_pairs={{0,32},{32,0},{1,33},{33,1},{2,34},{34,2},{3,35},{35,3},{4,36},{36... | collective-permute-start | bytes 4718600 | tf_op jit(solution)/shard_map/experts/ppermute | solution.py:181
  188.1 19.9 %collective-permute-start.14 = (bf16[128,3072]{1,0:T(8,128)(2,1)S(1)}, bf16[128,3072]{1,0:T(8,128)(2,1)S(1)}, u32[]{:S(2)}, u32[]{:S(2)}) collective-permute-start(bf16[128,3072]{1,0:T(8,128)(2,1)S(1)} %get-tuple-element.16), channel_id=1, source_target_pairs={{0,6},{2,0},{4,2},{6,4},{1,7},{3,1},{5,3},{7,5},{8,14},{10,8},{12,... | collective-permute-start | bytes 2359304 | tf_op jit(solution)/shard_map/combine/ppermute | solution.py:188
  192.2 19.9 %collective-permute-start.10 = (bf16[128,3072]{1,0:T(8,128)(2,1)S(1)}, bf16[128,3072]{1,0:T(8,128)(2,1)S(1)}, u32[]{:S(2)}, u32[]{:S(2)}) collective-permute-start(bf16[128,3072]{1,0:T(8,128)(2,1)S(1)} %get-tuple-element.15), channel_id=1, source_target_pairs={{0,2},{2,4},{4,6},{6,0},{1,3},{3,5},{5,7},{7,1},{8,10},{10,12},{12... | collective-permute-start | bytes 2359304 | tf_op jit(solution)/shard_map/combine/ppermute | solution.py:187
  193.7 19.8 %collective-permute-start.1 = (bf16[256,3072]{1,0:T(8,128)(2,1)S(1)}, bf16[256,3072]{1,0:T(8,128)(2,1)S(1)}, u32[]{:S(2)}, u32[]{:S(2)}) collective-permute-start(bf16[256,3072]{1,0:T(8,128)(2,1)S(1)} %convolution_convert_fusion.6), channel_id=1, source_target_pairs={{0,32},{32,0},{1,33},{33,1},{2,34},{34,2},{3,35},{35,3},{4,36},{36... | collective-permute-start | bytes 4718600 | tf_op jit(solution)/shard_map/experts/ppermute | solution.py:181
  208.7 35.9 %collective-permute-start.15 = (bf16[256,3072]{1,0:T(8,128)(2,1)S(1)}, bf16[256,3072]{1,0:T(8,128)(2,1)S(1)}, u32[]{:S(2)}, u32[]{:S(2)}) collective-permute-start(bf16[256,3072]{1,0:T(8,128)(2,1)S(1)} %add_convert_fusion.1), channel_id=1, source_target_pairs={{0,6},{2,0},{4,2},{6,4},{1,7},{3,1},{5,3},{7,5},{8,14},{10,8},{12,... | collective-permute-start | bytes 4718600 | tf_op jit(solution)/shard_map/combine/ppermute | solution.py:197
  212.8 35.6 %collective-permute-start.11 = (bf16[256,3072]{1,0:T(8,128)(2,1)S(1)}, bf16[256,3072]{1,0:T(8,128)(2,1)S(1)}, u32[]{:S(2)}, u32[]{:S(2)}) collective-permute-start(bf16[256,3072]{1,0:T(8,128)(2,1)S(1)} %add_convert_fusion.2), channel_id=1, source_target_pairs={{0,2},{2,4},{4,6},{6,0},{1,3},{3,5},{5,7},{7,1},{8,10},{10,12},{12... | collective-permute-start | bytes 4718600 | tf_op jit(solution)/shard_map/combine/ppermute | solution.py:196
  284.5 13.6 %all-to-all-start.2 = ((bf16[16,8,768]{2,1,0:T(8,128)(2,1)}), bf16[16,8,768]{2,1,0:T(8,128)(2,1)S(1)}, u32[]{:S(2)}, u32[]{:S(2)}) async-start(bf16[16,8,768]{2,1,0:T(8,128)(2,1)} %bitcast.227), calls=%async_computation.3 | async-start | bytes 393216 | tf_op jit(solution)/shard_map/combine/all_to_all | solution.py:206
  298.2 36.8 %copy-start.1 = (bf16[1,64,128]{2,1,0:T(8,128)(2,1)S(1)}, bf16[1,64,128]{2,1,0:T(8,128)(2,1)}, u32[]{:S(2)}) copy-start(bf16[1,64,128]{2,1,0:T(8,128)(2,1)} %param.19) | copy-start | bytes 49156
  (8 other events, 35.2 us)
Sparse Core Ops, SparseCore 0:
  76.0 36.0 all-gather.1
  250.7 33.7 reduce-scatter.1
